TPU v7x, 32 devices: a whole 2x2x4 slice. The times are simulated.
32 devices in a mesh: grp: 4 (over z), ep: 8 (over y, x, core).
Axes of the slice: x: 2, y: 2, z: 4, core: 2. Of those that a mesh axis runs over, the one named last changes fastest.
Arguments:
- resid: bfloat16 [8, 512, 2304], P('ep', 'grp'), may hold values from -6 to 6
- queries: bfloat16 [8, 512, 2304], P('ep', 'grp'), may hold values from -6 to 6
- keys: bfloat16 [8, 512, 2304], P('ep', 'grp'), may hold values from -6 to 6
- values: bfloat16 [8, 512, 2304], P('ep', 'grp'), may hold values from -6 to 6
- tenant: int32 [8, 512], P('ep', 'grp'), may hold values from 0 to 3, never falling along the last dimension, each value on 1 to 256 neighbouring positions
- out_proj: bfloat16 [2304, 2304], replicated, may hold values from -0.125 to 0.125
- norm_gain: float32 [2304], replicated, may hold values from 0.1 to 1.9
- router: bfloat16 [2304, 8], replicated, may hold values from -0.125 to 0.125
- routes: int32 [8, 512, 2], P('ep', 'grp'), may hold values from 0 to 7, all different within a row; in each aligned block of 128 rows (0 to 127, 128 to 255, ..., all dimensions but the last counted through in order) at most 40 rows name the same one
- expert_in: bfloat16 [8, 2304, 2, 5760], P('ep', None, None, 'grp'), as said below
- expert_out: bfloat16 [8, 5760, 2304], P('ep', 'grp'), as said below
Outputs:
- layer_out: bfloat16 [8, 512, 2304], P('ep', 'grp')
Inputs may be any that keep to these rules, and one draw needn't show every extreme that they name: Within each sequence tenant ids never fall; one tenant range spans exactly 256 positions. `routes`: the two experts of a token differ; in each aligned block of 128 tokens of one device no expert is named by more than 40 tokens, and some block names some expert exactly 40 times. `expert_in`: entries j and k with j == k // 1 are equal. `expert_out`: entries j and k with j == k // 1 are equal.
All inputs are finite; a program needn't handle non-finite values.
Results may differ from a plain program's by a relative error of at most 0.0056.
Values may be sent and summed in bfloat16 or wider, within the bound.
No kernel may reach another device: no remote copies, remote signals or barrier semaphores. Data moves between devices by JAX's collectives and lax.ppermute only.
A program may use at most 192 MiB of HBM per device.

v0:
```python
import jax
import jax.numpy as jnp
from jax import lax
from jax.sharding import PartitionSpec as P

HEADS = 36
HEAD_DIM = 64
EXPERTS = 8
TOP = 2


NEG = -1e30


def shift_up(x, first, last):
    return lax.ppermute(x, "grp", perm=[(i, i + 1) for i in range(first, last + 1)])


def shift_down(x, first, last):
    return lax.ppermute(x, "grp", perm=[(i, i - 1) for i in range(first, last + 1)])


def local(
    resid, queries, keys, values, tenant, out_proj, norm_gain, router, routes, expert_in, expert_out
):
    rows_here = resid.shape[1]
    width = resid.shape[2]
    n_ep = lax.axis_size("ep")
    n_grp = lax.axis_size("grp")
    seq_len = rows_here * n_grp
    replicas = n_ep // EXPERTS
    block = rows_here // replicas
    capacity = block * 5 // 16
    me_grp = lax.axis_index("grp")
    offset = me_grp * rows_here
    span = seq_len // 2
    back = min(n_grp - 1, -(-(span - 1) // rows_here))

    query_heads = queries[0].reshape(rows_here, HEADS, HEAD_DIM)
    query_pos = offset + jnp.arange(rows_here, dtype=jnp.int32)
    query_seg = tenant[0]
    scale = HEAD_DIM ** (-0.5)

    key_chunks = [keys[0]]
    value_chunks = [values[0]]
    seg_chunks = [tenant[0]]
    k_cur, v_cur, s_cur = keys[0], values[0], tenant[0]
    for _ in range(back):
        k_cur = shift_up(k_cur, 0, n_grp - 2)
        v_cur = shift_up(v_cur, 0, n_grp - 2)
        s_cur = shift_up(s_cur, 0, n_grp - 2)
        key_chunks.insert(0, k_cur)
        value_chunks.insert(0, v_cur)
        seg_chunks.insert(0, s_cur)
    key_piece = jnp.concatenate(key_chunks, axis=0)
    value_piece = jnp.concatenate(value_chunks, axis=0)
    seg_piece = jnp.concatenate(seg_chunks, axis=0)
    count = key_piece.shape[0]
    key_pos = offset - back * rows_here + jnp.arange(count, dtype=jnp.int32)
    key_heads = key_piece.reshape(count, HEADS, HEAD_DIM)
    value_heads = value_piece.reshape(count, HEADS, HEAD_DIM)
    scores = (
        jnp.einsum("qhd,khd->hqk", query_heads, key_heads, preferred_element_type=jnp.float32)
        * scale
    )
    allowed = (
        (query_pos[:, None] >= key_pos[None, :])
        & (key_pos[None, :] >= 0)
        & (query_seg[:, None] == seg_piece[None, :])
    )
    scores = jnp.where(allowed[None], scores, NEG)
    newest = jnp.max(scores, axis=-1)
    probs = jnp.where(allowed[None], jnp.exp(scores - newest[..., None]), 0.0)
    total = jnp.sum(probs, axis=-1)
    accum = jnp.einsum(
        "hqk,khd->hqd", probs.astype(jnp.bfloat16), value_heads, preferred_element_type=jnp.float32
    )
    attended = (
        jnp.transpose(accum / total[..., None], (1, 0, 2))
        .reshape(rows_here, width)
        .astype(jnp.bfloat16)
    )
    residual = resid[0].astype(jnp.float32) + jnp.dot(
        attended, out_proj, preferred_element_type=jnp.float32
    )
    normed = (
        residual
        * lax.rsqrt(jnp.mean(residual * residual, axis=-1, keepdims=True) + 1e-05)
        * norm_gain
    ).astype(jnp.bfloat16)
    logits = jnp.dot(normed, router, preferred_element_type=jnp.float32)
    local_routes = routes[0]
    expert_ids = jnp.arange(EXPERTS, dtype=jnp.int32)
    picked = jnp.sum(
        jnp.where(local_routes[:, :, None] == expert_ids[None, None, :], logits[:, None, :], 0.0),
        axis=-1,
    )
    gate_weights = jax.nn.softmax(picked, axis=-1).astype(jnp.bfloat16)
    half_id = jnp.arange(rows_here, dtype=jnp.int32) // block
    destination = local_routes * replicas + half_id[:, None]
    flat_dest = destination.reshape(-1)
    onehot = (flat_dest[:, None] == jnp.arange(n_ep, dtype=jnp.int32)[None, :]).astype(jnp.int32)
    earlier = jnp.cumsum(onehot, axis=0) - onehot
    position = jnp.sum(earlier * onehot, axis=1)
    slot = (flat_dest * capacity + position).reshape(rows_here, TOP)
    n_slots = n_ep * capacity
    matches = jnp.arange(n_slots, dtype=jnp.int32)[:, None, None] == slot[None]
    dispatch_table = jnp.any(matches, axis=-1).astype(jnp.bfloat16)
    outgoing = jnp.dot(dispatch_table, normed, preferred_element_type=jnp.float32).astype(
        jnp.bfloat16
    )
    outgoing = outgoing.reshape(n_ep, capacity, width)
    combine = jnp.transpose(
        jnp.sum(jnp.where(matches, gate_weights.astype(jnp.float32)[None], 0.0), axis=-1)
    ).astype(jnp.bfloat16)
    weight_in = expert_in[0]
    weight_out = expert_out[0]
    ff_here = weight_in.shape[2]
    weight_matrix = weight_in.reshape(width, 2 * ff_here)
    def expert(rows):
        both = jnp.dot(rows, weight_matrix, preferred_element_type=jnp.float32)
        hidden = (jax.nn.silu(both[:, :ff_here]) * both[:, ff_here:]).astype(jnp.bfloat16)
        return jnp.dot(hidden, weight_out, preferred_element_type=jnp.float32).astype(jnp.bfloat16)

    own = lax.all_to_all(outgoing, "ep", split_axis=0, concat_axis=0, tiled=True).reshape(
        n_slots, width
    )
    partial_own = expert(own)
    from_below, from_above = [None] * n_grp, [None] * n_grp
    up_rows, down_rows = own, own
    pending = []
    for r in range(1, n_grp):
        up_rows, down_rows, _ = lax.optimization_barrier((up_rows, down_rows, pending))
        pending = [partial_own] if r == 1 else [from_below[r - 1], from_above[r - 1]]
        up_rows = shift_up(up_rows, r - 1, n_grp - 2)
        down_rows = shift_down(down_rows, 1, n_grp - r)
        if 2 * r <= n_grp - 1:
            pair = expert(jnp.concatenate([up_rows, down_rows], axis=0))
            from_below[r], from_above[r] = pair[:n_slots], pair[n_slots:]
        else:
            chosen = jnp.where(me_grp >= r, up_rows, down_rows)
            from_below[r] = from_above[r] = expert(chosen)
    up_sum = down_sum = None
    for r in range(1, n_grp):
        send_up = from_above[n_grp - r]
        send_down = from_below[n_grp - r]
        if r == 1:
            send_up, send_down, _ = lax.optimization_barrier((send_up, send_down, pending))
        if r > 1:
            send_up = (send_up.astype(jnp.float32) + up_sum.astype(jnp.float32)).astype(
                jnp.bfloat16
            )
            send_down = (send_down.astype(jnp.float32) + down_sum.astype(jnp.float32)).astype(
                jnp.bfloat16
            )
        up_sum = shift_up(send_up, 0, r - 1)
        down_sum = shift_down(send_down, n_grp - r, n_grp - 1)
    expert_output = (
        partial_own.astype(jnp.float32) + up_sum.astype(jnp.float32) + down_sum.astype(jnp.float32)
    ).astype(jnp.bfloat16)
    summed = lax.all_to_all(
        expert_output.reshape(n_ep, capacity, width), "ep", split_axis=0, concat_axis=0, tiled=True
    ).reshape(n_slots, width)
    moe = jnp.dot(combine, summed, preferred_element_type=jnp.float32)
    return (residual + moe).astype(jnp.bfloat16)[None]


def solution(mesh):
    in_specs = (
        P("ep", "grp", None),
        P("ep", "grp", None),
        P("ep", "grp", None),
        P("ep", "grp", None),
        P("ep", "grp"),
        P(),
        P(),
        P(),
        P("ep", "grp", None),
        P("ep", None, None, "grp"),
        P("ep", "grp", None),
    )
    out_specs = P("ep", "grp", None)
    return jax.shard_map(local, mesh=mesh, in_specs=in_specs, out_specs=out_specs, check_vma=False)
```

profile of v0, /device:TPU:0, one launch (start us, length us, event | category | flops | bytes accessed | tf_op | source)
XLA Modules:
  0.0 351.7 jit_solution(3769439214499706144)
XLA Ops:
  0.0 5.9 %collective-permute-start.2 = (bf16[128,2304]{1,0:T(8,128)(2,1)}, bf16[128,2304]{1,0:T(8,128)(2,1)}, u32[]{:S(2)}, u32[]{:S(2)}) collective-permute-start(bf16[128,2304]{1,0:T(8,128)(2,1)} %bitcast.89), channel_id=1, source_target_pairs={{0,8},{8,16},{16,24},{1,9},{9,17},{17,25},{2,10},{10,18},{18,26},{... | collective-permute-start | bytes 1769480 | tf_op jit(solution)/shard_map/ppermute | solution.py:16
  19.1 5.2 %collective-permute-start.3 = (bf16[128,2304]{1,0:T(8,128)(2,1)}, bf16[128,2304]{1,0:T(8,128)(2,1)}, u32[]{:S(2)}, u32[]{:S(2)}) collective-permute-start(bf16[128,2304]{1,0:T(8,128)(2,1)} %collective-permute-done.2), channel_id=1, source_target_pairs={{0,8},{8,16},{16,24},{1,9},{9,17},{17,25},{2,10},{10,18},{18,26},{... | collective-permute-start | bytes 1769480 | tf_op jit(solution)/shard_map/ppermute | solution.py:16
  29.8 13.5 %collective-permute-done.1 = s32[128]{0:T(128)S(1)} collective-permute-done((s32[128]{0:T(128)S(1)}, s32[128]{0:T(128)S(1)}, u32[]{:S(2)}, u32[]{:S(2)}) %collective-permute-start.1) | collective-permute-done | bytes 544 | tf_op jit(solution)/shard_map/ppermute | solution.py:16
  45.9 5.2 %collective-permute-start.5 = (bf16[128,2304]{1,0:T(8,128)(2,1)S(1)}, bf16[128,2304]{1,0:T(8,128)(2,1)}, u32[]{:S(2)}, u32[]{:S(2)}) collective-permute-start(bf16[128,2304]{1,0:T(8,128)(2,1)S(1)} %collective-permute-done.4), channel_id=1, source_target_pairs={{0,8},{8,16},{16,24},{1,9},{9,17},{17,25},{2,10},{10,18},{18,26},{... | collective-permute-start | bytes 1769480 | tf_op jit(solution)/shard_map/ppermute | solution.py:16
  66.3 5.7 %multiply_reduce_fusion = (f32[128]{0:T(128)S(1)}, f32[128,2304]{1,0:T(8,128)S(1)}) fusion(bf16[128,2304]{0,1:T(8,128)(2,1)S(1)} %bitcast.88, bf16[2304,2304]{1,0:T(8,128)(2,1)} %param.16, bf16[1,128,2304]{2,1,0:T(8,128)(2,1)S(1)} %copy-done.5), kind=kOutput, calls=%fused_computation.65 | convolution fusion | flops 1360134016 | bytes 12976640 | tf_op jit(solution)/shard_map/dot_general | solution.py:83
  72.7 23.4 %all_to_all.10 = bf16[8,40,2304]{2,1,0:T(8,128)(2,1)S(1)} all-to-all(bf16[8,40,2304]{2,1,0:T(8,128)(2,1)S(1)} %bitcast.80), channel_id=1, replica_groups=mesh['grp'=4,'ep'=8] {'ep'}, dimensions={0} | all-to-all | bytes 2949120 | tf_op jit(solution)/shard_map/all_to_all | solution.py:125
  96.2 5.6 %collective-permute-start.6 = (bf16[320,2304]{1,0:T(8,128)(2,1)S(1)}, bf16[320,2304]{1,0:T(8,128)(2,1)}, u32[]{:S(2)}, u32[]{:S(2)}) collective-permute-start(bf16[320,2304]{1,0:T(8,128)(2,1)S(1)} %bitcast.85), channel_id=1, source_target_pairs={{0,8},{8,16},{16,24},{1,9},{9,17},{17,25},{2,10},{10,18},{18,26},{... | collective-permute-start | bytes 4423688 | tf_op jit(solution)/shard_map/ppermute | solution.py:16
  103.3 8.0 %fusion.91 = f32[320,2880]{1,0:T(8,128)S(1)} fusion(bf16[320,2304]{1,0:T(8,128)(2,1)S(1)} %bitcast.87, bf16[2304,2880]{0,1:T(8,128)(2,1)} %bitcast.98), kind=kOutput, calls=%fused_computation.110 | convolution fusion | flops 4246732800 | bytes 18432000 | tf_op jit(solution)/shard_map/dot_general | solution.py:121
  111.3 5.6 %fusion.13 = bf16[320,2304]{1,0:T(8,128)(2,1)S(1)} fusion(bf16[1,1440,2304]{2,1,0:T(8,128)(2,1)} %param.21, f32[320,2880]{1,0:T(8,128)S(1)} %fusion.91), kind=kOutput, calls=%fused_computation.13 | convolution fusion | flops 2126868480 | bytes 12042240 | tf_op jit(solution)/shard_map/dot_general | solution.py:123
  116.9 15.1 %collective-permute-done.6 = bf16[320,2304]{1,0:T(8,128)(2,1)} collective-permute-done((bf16[320,2304]{1,0:T(8,128)(2,1)S(1)}, bf16[320,2304]{1,0:T(8,128)(2,1)}, u32[]{:S(2)}, u32[]{:S(2)}) %collective-permute-start.6) | collective-permute-done | bytes 1474592 | tf_op jit(solution)/shard_map/ppermute | solution.py:16
  132.0 5.3 %collective-permute-done.7 = bf16[320,2304]{1,0:T(8,128)(2,1)} collective-permute-done((bf16[320,2304]{1,0:T(8,128)(2,1)S(1)}, bf16[320,2304]{1,0:T(8,128)(2,1)}, u32[]{:S(2)}, u32[]{:S(2)}) %collective-permute-start.7) | collective-permute-done | bytes 1474592 | tf_op jit(solution)/shard_map/ppermute | solution.py:20
  140.4 34.8 %collective-permute-done.9 = bf16[320,2304]{1,0:T(8,128)(2,1)} collective-permute-done((bf16[320,2304]{1,0:T(8,128)(2,1)}, bf16[320,2304]{1,0:T(8,128)(2,1)}, u32[]{:S(2)}, u32[]{:S(2)}) %collective-permute-start.9) | collective-permute-done | bytes 1474592 | tf_op jit(solution)/shard_map/ppermute | solution.py:20
  177.3 11.8 %fusion.54 = f32[320,2880]{1,0:T(8,128)} fusion(bf16[2304,2880]{0,1:T(8,128)(2,1)} %bitcast.99, bf16[320,2304]{1,0:T(8,128)(2,1)} %collective-permute-done.8, bf16[320,2304]{1,0:T(8,128)(2,1)} %collective-permute-done.9, pred[]{:T(512)S(6)} %ge.39), kind=kOutput, calls=%fused_computation.59 | convolution fusion | flops 4247470080 | bytes 19906560 | tf_op jit(solution)/shard_map/dot_general | solution.py:121
  189.1 6.8 %fusion.16 = bf16[320,2304]{1,0:T(8,128)(2,1)S(1)} fusion(bf16[1,1440,2304]{2,1,0:T(8,128)(2,1)} %param.21, f32[320,2880]{1,0:T(8,128)} %fusion.54), kind=kOutput, calls=%fused_computation.14 | convolution fusion | flops 2126868480 | bytes 12042240 | tf_op jit(solution)/shard_map/dot_general | solution.py:123
  195.9 13.9 %collective-permute-done.11 = bf16[320,2304]{1,0:T(8,128)(2,1)S(1)} collective-permute-done((bf16[320,2304]{1,0:T(8,128)(2,1)}, bf16[320,2304]{1,0:T(8,128)(2,1)S(1)}, u32[]{:S(2)}, u32[]{:S(2)}) %collective-permute-start.11) | collective-permute-done | bytes 1474592 | tf_op jit(solution)/shard_map/ppermute | solution.py:20
  209.8 10.2 %fusion.52 = f32[320,2880]{1,0:T(8,128)} fusion(bf16[2304,2880]{0,1:T(8,128)(2,1)} %bitcast.100, bf16[320,2304]{1,0:T(8,128)(2,1)S(1)} %collective-permute-done.10, bf16[320,2304]{1,0:T(8,128)(2,1)S(1)} %collective-permute-done.11, pred[]{:T(512)S(6)} %ge.40), kind=kOutput, calls=%fused_computation.57 | convolution fusion | flops 4247470080 | bytes 19906560 | tf_op jit(solution)/shard_map/dot_general | solution.py:121
  219.9 6.8 %fusion.19 = bf16[320,2304]{1,0:T(8,128)(2,1)S(1)} fusion(bf16[1,1440,2304]{2,1,0:T(8,128)(2,1)} %param.21, f32[320,2880]{1,0:T(8,128)} %fusion.52), kind=kOutput, calls=%fused_computation.15 | convolution fusion | flops 2126868480 | bytes 12042240 | tf_op jit(solution)/shard_map/dot_general | solution.py:123
  229.2 27.4 %collective-permute-done.12 = bf16[320,2304]{1,0:T(8,128)(2,1)S(1)} collective-permute-done((bf16[320,2304]{1,0:T(8,128)(2,1)S(1)}, bf16[320,2304]{1,0:T(8,128)(2,1)S(1)}, u32[]{:S(2)}, u32[]{:S(2)}) %collective-permute-start.12) | collective-permute-done | bytes 1474592 | tf_op jit(solution)/shard_map/ppermute | solution.py:16
  262.9 14.6 %fusion.32 = f32[640,2880]{0,1:T(8,128)S(1)} fusion(bf16[2304,2880]{0,1:T(8,128)(2,1)} %bitcast.101, bf16[320,2304]{1,0:T(8,128)(2,1)} %collective-permute-done.7, bf16[320,2304]{1,0:T(8,128)(2,1)} %collective-permute-done.6), kind=kOutput, calls=%fused_computation.32 | convolution fusion | flops 8499363840 | bytes 23592960 | tf_op jit(solution)/shard_map/dot_general | solution.py:121
  277.6 5.2 %fusion.10 = bf16[640,2304]{1,0:T(8,128)(2,1)S(1)} fusion(bf16[1,1440,2304]{2,1,0:T(8,128)(2,1)S(1)} %bitcast.103, f32[640,2880]{0,1:T(8,128)S(1)} %fusion.32), kind=kOutput, calls=%fused_computation.12 | convolution fusion | flops 4253736960 | bytes 16957440 | tf_op jit(solution)/shard_map/dot_general | solution.py:123
  282.8 6.3 %collective-permute-done.13 = bf16[320,2304]{1,0:T(8,128)(2,1)S(1)} collective-permute-done((bf16[320,2304]{1,0:T(8,128)(2,1)S(1)}, bf16[320,2304]{1,0:T(8,128)(2,1)S(1)}, u32[]{:S(2)}, u32[]{:S(2)}) %collective-permute-start.13) | collective-permute-done | bytes 1474592 | tf_op jit(solution)/shard_map/ppermute | solution.py:16
  291.2 7.3 %collective-permute-start.14 = (bf16[320,2304]{1,0:T(8,128)(2,1)S(1)}, bf16[320,2304]{1,0:T(8,128)(2,1)S(1)}, u32[]{:S(2)}, u32[]{:S(2)}) collective-permute-start(bf16[320,2304]{1,0:T(8,128)(2,1)S(1)} %get-tuple-element.21), channel_id=1, source_target_pairs={{0,8},{8,16},{16,24},{1,9},{9,17},{17,25},{2,10},{10,18},{18,26},{... | collective-permute-start | bytes 4423688 | tf_op jit(solution)/shard_map/ppermute | solution.py:16
  298.5 25.2 %collective-permute-done.17 = bf16[320,2304]{1,0:T(8,128)(2,1)S(1)} collective-permute-done((bf16[320,2304]{1,0:T(8,128)(2,1)S(1)}, bf16[320,2304]{1,0:T(8,128)(2,1)S(1)}, u32[]{:S(2)}, u32[]{:S(2)}) %collective-permute-start.17) | collective-permute-done | bytes 1474592 | tf_op jit(solution)/shard_map/ppermute | solution.py:20
  330.9 19.5 %all-to-all-done.1 = bf16[8,40,2304]{2,1,0:T(8,128)(2,1)S(1)} async-done(((bf16[8,40,2304]{2,1,0:T(8,128)(2,1)}), bf16[8,40,2304]{2,1,0:T(8,128)(2,1)S(1)}, u32[]{:S(2)}, u32[]{:S(2)}) %all-to-all-start.1) | async-done | bytes 1474592 | tf_op jit(solution)/shard_map/all_to_all | solution.py:161
  (95 shorter events, 62.8 us)
Async XLA Ops:
  0.0 330.4 %copy-start = (bf16[2304,8]{0,1:T(8,128)(2,1)S(1)}, bf16[2304,8]{0,1:T(8,128)(2,1)}, u32[]{:S(2)}) copy-start(bf16[2304,8]{0,1:T(8,128)(2,1)} %param.18) | copy-start | bytes 110596
  0.0 28.4 %copy-start.2 = (bf16[1,128,2304]{2,1,0:T(8,128)(2,1)S(1)}, bf16[1,128,2304]{2,1,0:T(8,128)(2,1)}, u32[]{:S(2)}) copy-start(bf16[1,128,2304]{2,1,0:T(8,128)(2,1)} %param.14) | copy-start | bytes 1769476
  0.0 29.5 %copy-start.1 = (bf16[1,128,2304]{2,1,0:T(8,128)(2,1)S(1)}, bf16[1,128,2304]{2,1,0:T(8,128)(2,1)}, u32[]{:S(2)}) copy-start(bf16[1,128,2304]{2,1,0:T(8,128)(2,1)} %param.12) | copy-start | bytes 1769476
  0.0 19.1 %collective-permute-start.2 = (bf16[128,2304]{1,0:T(8,128)(2,1)}, bf16[128,2304]{1,0:T(8,128)(2,1)}, u32[]{:S(2)}, u32[]{:S(2)}) collective-permute-start(bf16[128,2304]{1,0:T(8,128)(2,1)} %bitcast.89), channel_id=1, source_target_pairs={{0,8},{8,16},{16,24},{1,9},{9,17},{17,25},{2,10},{10,18},{18,26},{... | collective-permute-start | bytes 1769480 | tf_op jit(solution)/shard_map/ppermute | solution.py:16
  5.9 18.4 %collective-permute-start = (s32[128]{0:T(128)}, s32[128]{0:T(128)S(1)}, u32[]{:S(2)}, u32[]{:S(2)}) collective-permute-start(s32[128]{0:T(128)} %bitcast.95), channel_id=1, source_target_pairs={{0,8},{8,16},{16,24},{1,9},{9,17},{17,25},{2,10},{10,18},{18,26},{... | collective-permute-start | bytes 1544 | tf_op jit(solution)/shard_map/ppermute | solution.py:16
  8.6 36.3 %collective-permute-start.4 = (bf16[128,2304]{1,0:T(8,128)(2,1)}, bf16[128,2304]{1,0:T(8,128)(2,1)S(1)}, u32[]{:S(2)}, u32[]{:S(2)}) collective-permute-start(bf16[128,2304]{1,0:T(8,128)(2,1)} %bitcast.90), channel_id=1, source_target_pairs={{0,8},{8,16},{16,24},{1,9},{9,17},{17,25},{2,10},{10,18},{18,26},{... | collective-permute-start | bytes 1769480 | tf_op jit(solution)/shard_map/ppermute | solution.py:16
  14.1 29.2 %copy-start.8 = (s32[1,128]{1,0:T(1,128)S(1)}, s32[1,128]{1,0:T(1,128)}, u32[]{:S(2)}) copy-start(s32[1,128]{1,0:T(1,128)} %param.15) | copy-start | bytes 1540
  19.1 32.0 %collective-permute-start.3 = (bf16[128,2304]{1,0:T(8,128)(2,1)}, bf16[128,2304]{1,0:T(8,128)(2,1)}, u32[]{:S(2)}, u32[]{:S(2)}) collective-permute-start(bf16[128,2304]{1,0:T(8,128)(2,1)} %collective-permute-done.2), channel_id=1, source_target_pairs={{0,8},{8,16},{16,24},{1,9},{9,17},{17,25},{2,10},{10,18},{18,26},{... | collective-permute-start | bytes 1769480 | tf_op jit(solution)/shard_map/ppermute | solution.py:16
  24.3 18.9 %collective-permute-start.1 = (s32[128]{0:T(128)S(1)}, s32[128]{0:T(128)S(1)}, u32[]{:S(2)}, u32[]{:S(2)}) collective-permute-start(s32[128]{0:T(128)S(1)} %collective-permute-done), channel_id=1, source_target_pairs={{0,8},{8,16},{16,24},{1,9},{9,17},{17,25},{2,10},{10,18},{18,26},{... | collective-permute-start | bytes 1544 | tf_op jit(solution)/shard_map/ppermute | solution.py:16
  45.9 16.1 %collective-permute-start.5 = (bf16[128,2304]{1,0:T(8,128)(2,1)S(1)}, bf16[128,2304]{1,0:T(8,128)(2,1)}, u32[]{:S(2)}, u32[]{:S(2)}) collective-permute-start(bf16[128,2304]{1,0:T(8,128)(2,1)S(1)} %collective-permute-done.4), channel_id=1, source_target_pairs={{0,8},{8,16},{16,24},{1,9},{9,17},{17,25},{2,10},{10,18},{18,26},{... | collective-permute-start | bytes 1769480 | tf_op jit(solution)/shard_map/ppermute | solution.py:16
  96.2 35.8 %collective-permute-start.6 = (bf16[320,2304]{1,0:T(8,128)(2,1)S(1)}, bf16[320,2304]{1,0:T(8,128)(2,1)}, u32[]{:S(2)}, u32[]{:S(2)}) collective-permute-start(bf16[320,2304]{1,0:T(8,128)(2,1)S(1)} %bitcast.85), channel_id=1, source_target_pairs={{0,8},{8,16},{16,24},{1,9},{9,17},{17,25},{2,10},{10,18},{18,26},{... | collective-permute-start | bytes 4423688 | tf_op jit(solution)/shard_map/ppermute | solution.py:16
  101.8 35.5 %collective-permute-start.7 = (bf16[320,2304]{1,0:T(8,128)(2,1)S(1)}, bf16[320,2304]{1,0:T(8,128)(2,1)}, u32[]{:S(2)}, u32[]{:S(2)}) collective-permute-start(bf16[320,2304]{1,0:T(8,128)(2,1)S(1)} %bitcast.86), channel_id=1, source_target_pairs={{8,0},{16,8},{24,16},{9,1},{17,9},{25,17},{10,2},{18,10},{26,18},{... | collective-permute-start | bytes 4423688 | tf_op jit(solution)/shard_map/ppermute | solution.py:20
  137.3 3.1 collective-permute-start.8
  139.1 36.1 %collective-permute-start.9 = (bf16[320,2304]{1,0:T(8,128)(2,1)}, bf16[320,2304]{1,0:T(8,128)(2,1)}, u32[]{:S(2)}, u32[]{:S(2)}) collective-permute-start(bf16[320,2304]{1,0:T(8,128)(2,1)} %collective-permute-done.7), channel_id=1, source_target_pairs={{8,0},{16,8},{9,1},{17,9},{10,2},{18,10},{11,3},{19,11},{12,4},{20... | collective-permute-start | bytes 4423688 | tf_op jit(solution)/shard_map/ppermute | solution.py:20
  175.2 20.7 %collective-permute-start.10 = (bf16[320,2304]{1,0:T(8,128)(2,1)}, bf16[320,2304]{1,0:T(8,128)(2,1)S(1)}, u32[]{:S(2)}, u32[]{:S(2)}) collective-permute-start(bf16[320,2304]{1,0:T(8,128)(2,1)} %collective-permute-done.8), channel_id=1, source_target_pairs={{16,24},{17,25},{18,26},{19,27},{20,28},{21,29},{22,30},{23,31}} | collective-permute-start | bytes 4423688 | tf_op jit(solution)/shard_map/ppermute | solution.py:16
  176.0 33.8 %collective-permute-start.11 = (bf16[320,2304]{1,0:T(8,128)(2,1)}, bf16[320,2304]{1,0:T(8,128)(2,1)S(1)}, u32[]{:S(2)}, u32[]{:S(2)}) collective-permute-start(bf16[320,2304]{1,0:T(8,128)(2,1)} %collective-permute-done.9), channel_id=1, source_target_pairs={{8,0},{9,1},{10,2},{11,3},{12,4},{13,5},{14,6},{15,7}} | collective-permute-start | bytes 4423688 | tf_op jit(solution)/shard_map/ppermute | solution.py:20
  226.8 29.9 %collective-permute-start.12 = (bf16[320,2304]{1,0:T(8,128)(2,1)S(1)}, bf16[320,2304]{1,0:T(8,128)(2,1)S(1)}, u32[]{:S(2)}, u32[]{:S(2)}) collective-permute-start(bf16[320,2304]{1,0:T(8,128)(2,1)S(1)} %fusion.19), channel_id=1, source_target_pairs={{0,8},{1,9},{2,10},{3,11},{4,12},{5,13},{6,14},{7,15}} | collective-permute-start | bytes 4423688 | tf_op jit(solution)/shard_map/ppermute | solution.py:16
  228.4 28.2 %collective-permute-start.15 = (bf16[320,2304]{1,0:T(8,128)(2,1)S(1)}, bf16[320,2304]{1,0:T(8,128)(2,1)S(1)}, u32[]{:S(2)}, u32[]{:S(2)}) collective-permute-start(bf16[320,2304]{1,0:T(8,128)(2,1)S(1)} %fusion.19), channel_id=1, source_target_pairs={{24,16},{25,17},{26,18},{27,19},{28,20},{29,21},{30,22},{31,23}} | collective-permute-start | bytes 4423688 | tf_op jit(solution)/shard_map/ppermute | solution.py:20
  257.3 31.8 %collective-permute-start.13 = (bf16[320,2304]{1,0:T(8,128)(2,1)S(1)}, bf16[320,2304]{1,0:T(8,128)(2,1)S(1)}, u32[]{:S(2)}, u32[]{:S(2)}) collective-permute-start(bf16[320,2304]{1,0:T(8,128)(2,1)S(1)} %get-tuple-element.23), channel_id=1, source_target_pairs={{0,8},{8,16},{1,9},{9,17},{2,10},{10,18},{3,11},{11,19},{4,12},{12... | collective-permute-start | bytes 4423688 | tf_op jit(solution)/shard_map/ppermute | solution.py:16
  261.8 15.7 %slice-start = ((s8[6635520]{0:T(1024)(128)(4,1)}), s8[4194304]{0:T(1024)(128)(4,1)S(1)}, s32[]{:S(2)}) async-start(s8[6635520]{0:T(1024)(128)(4,1)} %bitcast.102), calls=%async_computation.2 | async-start | bytes 8388608
  261.8 27.3 %collective-permute-start.16 = (bf16[320,2304]{1,0:T(8,128)(2,1)S(1)}, bf16[320,2304]{1,0:T(8,128)(2,1)S(1)}, u32[]{:S(2)}, u32[]{:S(2)}) collective-permute-start(bf16[320,2304]{1,0:T(8,128)(2,1)S(1)} %get-tuple-element.24), channel_id=1, source_target_pairs={{16,8},{24,16},{17,9},{25,17},{18,10},{26,18},{19,11},{27,19},{20,... | collective-permute-start | bytes 4423688 | tf_op jit(solution)/shard_map/ppermute | solution.py:20
  289.9 33.8 %collective-permute-start.17 = (bf16[320,2304]{1,0:T(8,128)(2,1)S(1)}, bf16[320,2304]{1,0:T(8,128)(2,1)S(1)}, u32[]{:S(2)}, u32[]{:S(2)}) collective-permute-start(bf16[320,2304]{1,0:T(8,128)(2,1)S(1)} %get-tuple-element.22), channel_id=1, source_target_pairs={{8,0},{16,8},{24,16},{9,1},{17,9},{25,17},{10,2},{18,10},{26,18},{... | collective-permute-start | bytes 4423688 | tf_op jit(solution)/shard_map/ppermute | solution.py:20
  291.2 33.7 %collective-permute-start.14 = (bf16[320,2304]{1,0:T(8,128)(2,1)S(1)}, bf16[320,2304]{1,0:T(8,128)(2,1)S(1)}, u32[]{:S(2)}, u32[]{:S(2)}) collective-permute-start(bf16[320,2304]{1,0:T(8,128)(2,1)S(1)} %get-tuple-element.21), channel_id=1, source_target_pairs={{0,8},{8,16},{16,24},{1,9},{9,17},{17,25},{2,10},{10,18},{18,26},{... | collective-permute-start | bytes 4423688 | tf_op jit(solution)/shard_map/ppermute | solution.py:16
  326.6 23.8 %all-to-all-start.1 = ((bf16[8,40,2304]{2,1,0:T(8,128)(2,1)}), bf16[8,40,2304]{2,1,0:T(8,128)(2,1)S(1)}, u32[]{:S(2)}, u32[]{:S(2)}) async-start(bf16[8,40,2304]{2,1,0:T(8,128)(2,1)} %bitcast.79), calls=%async_computation.1 | async-start | bytes 2949120 | tf_op jit(solution)/shard_map/all_to_all | solution.py:161
  (6 other events, 48.0 us)
where the time goes:
time: 353 us; the launch traced here: 352 us
  waiting for transfers between devices  170 us (48%)
  matrix products  81.1 us (23%)
  starting transfers between devices  57.7 us (16%)
  blocking collectives  23.4 us (7%)
  local copies, waits for them, and re-layouts  9.86 us (3%)
  other arithmetic  9.23 us (3%)
    ppermute x6, waiting for transfers between devices, shift_down(): lax.ppermute(x, 'grp', perm=[(i, i - 1) for i in range(first, last + 1)])  79.2 us
    ppermute x12, waiting for transfers between devices, shift_up(): lax.ppermute(x, 'grp', perm=[(i, i + 1) for i in range(first, last + 1)])  71.2 us
    ppermute x12, starting transfers between devices, shift_up(): lax.ppermute(x, 'grp', perm=[(i, i + 1) for i in range(first, last + 1)])  46.7 us
    dot_general x4, matrix products, expert(): both = jnp.dot(rows, weight_matrix, preferred_element_type=jnp.float32)  44.6 us
    dot_general x4, matrix products, expert(): jnp.dot(hidden, weight_out, preferred_element_type=jnp.float32)  24.4 us
    all_to_all x1, blocking collectives, local(): lax.all_to_all(outgoing, 'ep', split_axis=0, concat_axis=0, tiled=True)  23.4 us
    all_to_all x1, waiting for transfers between devices, local(): lax.all_to_all(expert_output.reshape(n_ep, capacity, width), 'ep', split_...  19.5 us
    ppermute x6, starting transfers between devices, shift_down(): lax.ppermute(x, 'grp', perm=[(i, i - 1) for i in range(first, last + 1)])  7.19 us
  transfers between devices with their start and end apart: 19, of which 12 were waited for; matrix products, arithmetic and copies ran while one was open for 19% of the time, Pallas kernels for 0%

commit v1 on v0

--- a/solution.py
+++ b/solution.py
@@ -139,20 +139,22 @@
             from_below[r], from_above[r] = pair[:n_slots], pair[n_slots:]
         else:
             chosen = jnp.where(me_grp >= r, up_rows, down_rows)
-            from_below[r] = from_above[r] = expert(chosen)
-    up_sum = down_sum = None
-    for r in range(1, n_grp):
-        send_up = from_above[n_grp - r]
-        send_down = from_below[n_grp - r]
-        if r == 1:
-            send_up, send_down, _ = lax.optimization_barrier((send_up, send_down, pending))
-        if r > 1:
-            send_up = (send_up.astype(jnp.float32) + up_sum.astype(jnp.float32)).astype(
-                jnp.bfloat16
-            )
-            send_down = (send_down.astype(jnp.float32) + down_sum.astype(jnp.float32)).astype(
-                jnp.bfloat16
-            )
+            if r == n_grp - 1:
+                half = n_slots // 2
+                last_halves = [expert(chosen[:half]), expert(chosen[half:])]
+            else:
+                from_below[r] = from_above[r] = expert(chosen)
+    up_sum = jnp.concatenate([shift_up(h, 0, 0) for h in last_halves], axis=0)
+    down_sum = jnp.concatenate(
+        [shift_down(h, n_grp - 1, n_grp - 1) for h in last_halves], axis=0
+    )
+    for r in range(2, n_grp):
+        send_up = (from_above[n_grp - r].astype(jnp.float32) + up_sum.astype(jnp.float32)).astype(
+            jnp.bfloat16
+        )
+        send_down = (
+            from_below[n_grp - r].astype(jnp.float32) + down_sum.astype(jnp.float32)
+        ).astype(jnp.bfloat16)
         up_sum = shift_up(send_up, 0, r - 1)
         down_sum = shift_down(send_down, n_grp - r, n_grp - 1)
     expert_output = (

time: 353 us -> 378 us (1.071); the launches traced: 352 us -> 372 us
  matrix products: 81.1 us -> 101 us
  waiting for transfers between devices: 170 us -> 158 us
  starting transfers between devices: 57.7 us -> 69.4 us
    ppermute x12 -> x13, waiting for transfers between devices: 71.2 us -> 39.9 us  [shift_up(): lax.ppermute(x, 'grp', perm=[(i, i + 1) for i in range(first, last + 1)])]
    ppermute x6 -> x7, waiting for transfers between devices: 79.2 us -> 98.5 us  [shift_down(): lax.ppermute(x, 'grp', perm=[(i, i - 1) for i in range(first, last + 1)])]
    ppermute x6 -> x7, starting transfers between devices: 7.19 us -> 21.3 us  [shift_down(): lax.ppermute(x, 'grp', perm=[(i, i - 1) for i in range(first, last + 1)])]
    dot_general x4 -> x5, matrix products: 24.4 us -> 35.1 us  [expert(): jnp.dot(hidden, weight_out, preferred_element_type=jnp.float32)]
    dot_general x4 -> x5, matrix products: 44.6 us -> 53.5 us  [expert(): both = jnp.dot(rows, weight_matrix, preferred_element_type=jnp.float32)]
    ppermute x12 -> x13, starting transfers between devices: 46.7 us -> 44.3 us  [shift_up(): lax.ppermute(x, 'grp', perm=[(i, i + 1) for i in range(first, last + 1)])]
  transfers between devices with their start and end apart: 19 -> 21, of which waited for: 12 -> 11; matrix products, arithmetic and copies ran while one was open for 19% -> 20% of each run, Pallas kernels for 0% -> 0%
where the time goes in v1:
time: 378 us; the launch traced here: 372 us
  waiting for transfers between devices  158 us (42%)
  matrix products  101 us (27%)
  starting transfers between devices  69.4 us (18%)
  blocking collectives  23.5 us (6%)
  other arithmetic  10.1 us (3%)
  local copies, waits for them, and re-layouts  9.87 us (3%)
    ppermute x7, waiting for transfers between devices, shift_down(): lax.ppermute(x, 'grp', perm=[(i, i - 1) for i in range(first, last + 1)])  98.5 us
    dot_general x5, matrix products, expert(): both = jnp.dot(rows, weight_matrix, preferred_element_type=jnp.float32)  53.5 us
    ppermute x13, starting transfers between devices, shift_up(): lax.ppermute(x, 'grp', perm=[(i, i + 1) for i in range(first, last + 1)])  44.3 us
    ppermute x13, waiting for transfers between devices, shift_up(): lax.ppermute(x, 'grp', perm=[(i, i + 1) for i in range(first, last + 1)])  39.9 us
    dot_general x5, matrix products, expert(): jnp.dot(hidden, weight_out, preferred_element_type=jnp.float32)  35.1 us
    all_to_all x1, blocking collectives, local(): lax.all_to_all(outgoing, 'ep', split_axis=0, concat_axis=0, tiled=True)  23.5 us
    ppermute x7, starting transfers between devices, shift_down(): lax.ppermute(x, 'grp', perm=[(i, i - 1) for i in range(first, last + 1)])  21.3 us
    all_to_all x1, waiting for transfers between devices, local(): lax.all_to_all(expert_output.reshape(n_ep, capacity, width), 'ep', split_...  19.4 us
  transfers between devices with their start and end apart: 21, of which 11 were waited for; matrix products, arithmetic and copies ran while one was open for 20% of the time, Pallas kernels for 0%

profile of v1, /device:TPU:0, one launch (start us, length us, event | category | flops | bytes accessed | tf_op | source)
XLA Modules:
  0.0 371.9 jit_solution(17653142881786719821)
XLA Ops:
  0.0 5.9 %collective-permute-start.2 = (bf16[128,2304]{1,0:T(8,128)(2,1)}, bf16[128,2304]{1,0:T(8,128)(2,1)}, u32[]{:S(2)}, u32[]{:S(2)}) collective-permute-start(bf16[128,2304]{1,0:T(8,128)(2,1)} %bitcast.105), channel_id=1, source_target_pairs={{0,8},{8,16},{16,24},{1,9},{9,17},{17,25},{2,10},{10,18},{18,26},{... | collective-permute-start | bytes 1769480 | tf_op jit(solution)/shard_map/ppermute | solution.py:16
  19.1 5.2 %collective-permute-start.3 = (bf16[128,2304]{1,0:T(8,128)(2,1)}, bf16[128,2304]{1,0:T(8,128)(2,1)}, u32[]{:S(2)}, u32[]{:S(2)}) collective-permute-start(bf16[128,2304]{1,0:T(8,128)(2,1)} %collective-permute-done.2), channel_id=1, source_target_pairs={{0,8},{8,16},{16,24},{1,9},{9,17},{17,25},{2,10},{10,18},{18,26},{... | collective-permute-start | bytes 1769480 | tf_op jit(solution)/shard_map/ppermute | solution.py:16
  29.8 13.5 %collective-permute-done.1 = s32[128]{0:T(128)S(1)} collective-permute-done((s32[128]{0:T(128)S(1)}, s32[128]{0:T(128)S(1)}, u32[]{:S(2)}, u32[]{:S(2)}) %collective-permute-start.1) | collective-permute-done | bytes 544 | tf_op jit(solution)/shard_map/ppermute | solution.py:16
  45.9 5.2 %collective-permute-start.5 = (bf16[128,2304]{1,0:T(8,128)(2,1)S(1)}, bf16[128,2304]{1,0:T(8,128)(2,1)}, u32[]{:S(2)}, u32[]{:S(2)}) collective-permute-start(bf16[128,2304]{1,0:T(8,128)(2,1)S(1)} %collective-permute-done.4), channel_id=1, source_target_pairs={{0,8},{8,16},{16,24},{1,9},{9,17},{17,25},{2,10},{10,18},{18,26},{... | collective-permute-start | bytes 1769480 | tf_op jit(solution)/shard_map/ppermute | solution.py:16
  66.3 5.7 %multiply_reduce_fusion = (f32[128]{0:T(128)S(1)}, f32[128,2304]{1,0:T(8,128)S(1)}) fusion(bf16[128,2304]{0,1:T(8,128)(2,1)S(1)} %bitcast.104, bf16[2304,2304]{1,0:T(8,128)(2,1)} %param.16, bf16[1,128,2304]{2,1,0:T(8,128)(2,1)S(1)} %copy-done.5), kind=kOutput, calls=%fused_computation.63 | convolution fusion | flops 1360134016 | bytes 12976640 | tf_op jit(solution)/shard_map/dot_general | solution.py:83
  72.7 23.5 %all_to_all.10 = bf16[8,40,2304]{2,1,0:T(8,128)(2,1)S(1)} all-to-all(bf16[8,40,2304]{2,1,0:T(8,128)(2,1)S(1)} %bitcast.96), channel_id=1, replica_groups=mesh['grp'=4,'ep'=8] {'ep'}, dimensions={0} | all-to-all | bytes 2949120 | tf_op jit(solution)/shard_map/all_to_all | solution.py:125
  102.3 10.2 %fusion.102 = f32[320,2880]{1,0:T(8,128)} fusion(bf16[320,2304]{1,0:T(8,128)(2,1)S(1)} %bitcast.103, bf16[2304,2880]{0,1:T(8,128)(2,1)} %bitcast.87), kind=kOutput, calls=%fused_computation.118 | convolution fusion | flops 4246732800 | bytes 18432000 | tf_op jit(solution)/shard_map/dot_general | solution.py:121
  112.5 6.8 %fusion.15 = bf16[320,2304]{1,0:T(8,128)(2,1)S(1)} fusion(bf16[1,1440,2304]{2,1,0:T(8,128)(2,1)} %param.21, f32[320,2880]{1,0:T(8,128)} %fusion.102), kind=kOutput, calls=%fused_computation.15 | convolution fusion | flops 2126868480 | bytes 12042240 | tf_op jit(solution)/shard_map/dot_general | solution.py:123
  119.3 12.7 %collective-permute-done.6 = bf16[320,2304]{1,0:T(8,128)(2,1)S(1)} collective-permute-done((bf16[320,2304]{1,0:T(8,128)(2,1)S(1)}, bf16[320,2304]{1,0:T(8,128)(2,1)S(1)}, u32[]{:S(2)}, u32[]{:S(2)}) %collective-permute-start.6) | collective-permute-done | bytes 1474592 | tf_op jit(solution)/shard_map/ppermute | solution.py:16
  139.3 35.6 %collective-permute-done.9 = bf16[320,2304]{1,0:T(8,128)(2,1)} collective-permute-done((bf16[320,2304]{1,0:T(8,128)(2,1)S(1)}, bf16[320,2304]{1,0:T(8,128)(2,1)}, u32[]{:S(2)}, u32[]{:S(2)}) %collective-permute-start.9) | collective-permute-done | bytes 1474592 | tf_op jit(solution)/shard_map/ppermute | solution.py:20
  178.0 32.6 %collective-permute-done.11 = bf16[320,2304]{1,0:T(8,128)(2,1)} collective-permute-done((bf16[320,2304]{1,0:T(8,128)(2,1)}, bf16[320,2304]{1,0:T(8,128)(2,1)}, u32[]{:S(2)}, u32[]{:S(2)}) %collective-permute-start.11) | collective-permute-done | bytes 1474592 | tf_op jit(solution)/shard_map/ppermute | solution.py:20
  212.1 9.3 %fusion.75 = f32[160,2880]{1,0:T(8,128)S(1)} fusion(bf16[2304,2880]{0,1:T(8,128)(2,1)} %bitcast.88, bf16[320,2304]{1,0:T(8,128)(2,1)S(1)} %broadcast_select_fusion), kind=kOutput, calls=%fused_computation.71 | convolution fusion | flops 2123366400 | bytes 15851520 | tf_op jit(solution)/shard_map/dot_general | solution.py:121
  221.4 9.3 %fusion.77 = f32[160,2880]{1,0:T(8,128)S(1)} fusion(bf16[2304,2880]{0,1:T(8,128)(2,1)} %bitcast.89, bf16[320,2304]{1,0:T(8,128)(2,1)S(1)} %broadcast_select_fusion), kind=kOutput, calls=%fused_computation.73 | convolution fusion | flops 2123366400 | bytes 15851520 | tf_op jit(solution)/shard_map/dot_general | solution.py:121
  230.7 5.3 %fusion.28 = bf16[160,2304]{1,0:T(8,128)(2,1)} fusion(bf16[1,1440,2304]{2,1,0:T(8,128)(2,1)} %param.21, f32[160,2880]{1,0:T(8,128)S(1)} %fusion.75), kind=kOutput, calls=%fused_computation.24 | convolution fusion | flops 1063434240 | bytes 9338880 | tf_op jit(solution)/shard_map/dot_general | solution.py:123
  239.8 5.3 %fusion.25 = bf16[160,2304]{1,0:T(8,128)(2,1)} fusion(bf16[1,1440,2304]{2,1,0:T(8,128)(2,1)} %param.21, f32[160,2880]{1,0:T(8,128)S(1)} %fusion.77), kind=kOutput, calls=%fused_computation.23 | convolution fusion | flops 1063434240 | bytes 9338880 | tf_op jit(solution)/shard_map/dot_general | solution.py:123
  247.2 13.7 %collective-permute-start.16 = (bf16[160,2304]{1,0:T(8,128)(2,1)}, bf16[160,2304]{1,0:T(8,128)(2,1)}, u32[]{:S(2)}, u32[]{:S(2)}) collective-permute-start(bf16[160,2304]{1,0:T(8,128)(2,1)} %fusion.25), channel_id=1, source_target_pairs={{24,16},{25,17},{26,18},{27,19},{28,20},{29,21},{30,22},{31,23}} | collective-permute-start | bytes 2211848 | tf_op jit(solution)/shard_map/ppermute | solution.py:20
  260.9 12.0 %fusion.57 = f32[320,2880]{1,0:T(8,128)} fusion(bf16[2304,2880]{0,1:T(8,128)(2,1)} %bitcast.90, bf16[320,2304]{1,0:T(8,128)(2,1)} %collective-permute-done.8, bf16[320,2304]{1,0:T(8,128)(2,1)} %collective-permute-done.9, pred[]{:T(512)S(6)} %ge.39), kind=kOutput, calls=%fused_computation.57 | convolution fusion | flops 4247470080 | bytes 19906560 | tf_op jit(solution)/shard_map/dot_general | solution.py:121
  272.9 7.8 %add_convert_fusion.4 = (bf16[320,2304]{1,0:T(8,128)(2,1)S(1)}, bf16[320,2304]{1,0:T(8,128)(2,1)S(1)}) fusion(bf16[160,2304]{1,0:T(8,128)(2,1)} %collective-permute-done.13, bf16[160,2304]{1,0:T(8,128)(2,1)} %collective-permute-done.12, bf16[160,2304]{1,0:T(8,128)(2,1)} %collective-permute-done.17, bf16[160,2304]{1,0:T(8,128)(2,1)} %collective-permute-done.16, ...), kind=kOutput, calls=%fused_computation.40 | convolution fusion | flops 2136453120 | bytes 16465920 | tf_op jit(solution)/shard_map/dot_general | solution.py:123
  283.0 12.8 %fusion.38 = f32[640,2880]{0,1:T(8,128)} fusion(bf16[2304,2880]{0,1:T(8,128)(2,1)S(1)} %bitcast.93, bf16[320,2304]{1,0:T(8,128)(2,1)S(1)} %copy-done.12, bf16[320,2304]{1,0:T(8,128)(2,1)S(1)} %copy-done.10), kind=kOutput, calls=%fused_computation.32 | convolution fusion | flops 8499363840 | bytes 23592960 | tf_op jit(solution)/shard_map/dot_general | solution.py:121
  295.7 9.9 %fusion.12 = bf16[640,2304]{1,0:T(8,128)(2,1)S(1)} fusion(bf16[1,1440,2304]{2,1,0:T(8,128)(2,1)} %param.21, f32[640,2880]{0,1:T(8,128)} %fusion.38), kind=kOutput, calls=%fused_computation.14 | convolution fusion | flops 4253736960 | bytes 16957440 | tf_op jit(solution)/shard_map/dot_general | solution.py:123
  305.7 4.8 %collective-permute-done.14 = bf16[320,2304]{1,0:T(8,128)(2,1)S(1)} collective-permute-done((bf16[320,2304]{1,0:T(8,128)(2,1)S(1)}, bf16[320,2304]{1,0:T(8,128)(2,1)S(1)}, u32[]{:S(2)}, u32[]{:S(2)}) %collective-permute-start.14) | collective-permute-done | bytes 1474592 | tf_op jit(solution)/shard_map/ppermute | solution.py:16
  312.5 5.2 %collective-permute-start.15 = (bf16[320,2304]{1,0:T(8,128)(2,1)S(1)}, bf16[320,2304]{1,0:T(8,128)(2,1)S(1)}, u32[]{:S(2)}, u32[]{:S(2)}) collective-permute-start(bf16[320,2304]{1,0:T(8,128)(2,1)S(1)} %get-tuple-element.17), channel_id=1, source_target_pairs={{0,8},{8,16},{16,24},{1,9},{9,17},{17,25},{2,10},{10,18},{18,26},{... | collective-permute-start | bytes 4423688 | tf_op jit(solution)/shard_map/ppermute | solution.py:16
  317.7 26.1 %collective-permute-done.19 = bf16[320,2304]{1,0:T(8,128)(2,1)S(1)} collective-permute-done((bf16[320,2304]{1,0:T(8,128)(2,1)S(1)}, bf16[320,2304]{1,0:T(8,128)(2,1)S(1)}, u32[]{:S(2)}, u32[]{:S(2)}) %collective-permute-start.19) | collective-permute-done | bytes 1474592 | tf_op jit(solution)/shard_map/ppermute | solution.py:20
  351.0 19.4 %all-to-all-done.1 = bf16[8,40,2304]{2,1,0:T(8,128)(2,1)S(1)} async-done(((bf16[8,40,2304]{2,1,0:T(8,128)(2,1)}), bf16[8,40,2304]{2,1,0:T(8,128)(2,1)S(1)}, u32[]{:S(2)}, u32[]{:S(2)}) %all-to-all-start.1) | async-done | bytes 1474592 | tf_op jit(solution)/shard_map/all_to_all | solution.py:163
  (113 shorter events, 73.6 us)
Async XLA Ops:
  0.0 350.5 %copy-start = (bf16[2304,8]{0,1:T(8,128)(2,1)S(1)}, bf16[2304,8]{0,1:T(8,128)(2,1)}, u32[]{:S(2)}) copy-start(bf16[2304,8]{0,1:T(8,128)(2,1)} %param.18) | copy-start | bytes 110596
  0.0 29.5 %copy-start.1 = (bf16[1,128,2304]{2,1,0:T(8,128)(2,1)S(1)}, bf16[1,128,2304]{2,1,0:T(8,128)(2,1)}, u32[]{:S(2)}) copy-start(bf16[1,128,2304]{2,1,0:T(8,128)(2,1)} %param.12) | copy-start | bytes 1769476
  0.0 19.1 %collective-permute-start.2 = (bf16[128,2304]{1,0:T(8,128)(2,1)}, bf16[128,2304]{1,0:T(8,128)(2,1)}, u32[]{:S(2)}, u32[]{:S(2)}) collective-permute-start(bf16[128,2304]{1,0:T(8,128)(2,1)} %bitcast.105), channel_id=1, source_target_pairs={{0,8},{8,16},{16,24},{1,9},{9,17},{17,25},{2,10},{10,18},{18,26},{... | collective-permute-start | bytes 1769480 | tf_op jit(solution)/shard_map/ppermute | solution.py:16
  5.9 18.4 %collective-permute-start = (s32[128]{0:T(128)}, s32[128]{0:T(128)S(1)}, u32[]{:S(2)}, u32[]{:S(2)}) collective-permute-start(s32[128]{0:T(128)} %bitcast.111), channel_id=1, source_target_pairs={{0,8},{8,16},{16,24},{1,9},{9,17},{17,25},{2,10},{10,18},{18,26},{... | collective-permute-start | bytes 1544 | tf_op jit(solution)/shard_map/ppermute | solution.py:16
  8.6 36.3 %collective-permute-start.4 = (bf16[128,2304]{1,0:T(8,128)(2,1)}, bf16[128,2304]{1,0:T(8,128)(2,1)S(1)}, u32[]{:S(2)}, u32[]{:S(2)}) collective-permute-start(bf16[128,2304]{1,0:T(8,128)(2,1)} %bitcast.106), channel_id=1, source_target_pairs={{0,8},{8,16},{16,24},{1,9},{9,17},{17,25},{2,10},{10,18},{18,26},{... | collective-permute-start | bytes 1769480 | tf_op jit(solution)/shard_map/ppermute | solution.py:16
  14.1 29.2 %copy-start.8 = (s32[1,128]{1,0:T(1,128)S(1)}, s32[1,128]{1,0:T(1,128)}, u32[]{:S(2)}) copy-start(s32[1,128]{1,0:T(1,128)} %param.15) | copy-start | bytes 1540
  19.1 32.0 %collective-permute-start.3 = (bf16[128,2304]{1,0:T(8,128)(2,1)}, bf16[128,2304]{1,0:T(8,128)(2,1)}, u32[]{:S(2)}, u32[]{:S(2)}) collective-permute-start(bf16[128,2304]{1,0:T(8,128)(2,1)} %collective-permute-done.2), channel_id=1, source_target_pairs={{0,8},{8,16},{16,24},{1,9},{9,17},{17,25},{2,10},{10,18},{18,26},{... | collective-permute-start | bytes 1769480 | tf_op jit(solution)/shard_map/ppermute | solution.py:16
  24.3 18.9 %collective-permute-start.1 = (s32[128]{0:T(128)S(1)}, s32[128]{0:T(128)S(1)}, u32[]{:S(2)}, u32[]{:S(2)}) collective-permute-start(s32[128]{0:T(128)S(1)} %collective-permute-done), channel_id=1, source_target_pairs={{0,8},{8,16},{16,24},{1,9},{9,17},{17,25},{2,10},{10,18},{18,26},{... | collective-permute-start | bytes 1544 | tf_op jit(solution)/shard_map/ppermute | solution.py:16
  45.9 16.1 %collective-permute-start.5 = (bf16[128,2304]{1,0:T(8,128)(2,1)S(1)}, bf16[128,2304]{1,0:T(8,128)(2,1)}, u32[]{:S(2)}, u32[]{:S(2)}) collective-permute-start(bf16[128,2304]{1,0:T(8,128)(2,1)S(1)} %collective-permute-done.4), channel_id=1, source_target_pairs={{0,8},{8,16},{16,24},{1,9},{9,17},{17,25},{2,10},{10,18},{18,26},{... | collective-permute-start | bytes 1769480 | tf_op jit(solution)/shard_map/ppermute | solution.py:16
  96.2 35.8 %collective-permute-start.6 = (bf16[320,2304]{1,0:T(8,128)(2,1)S(1)}, bf16[320,2304]{1,0:T(8,128)(2,1)S(1)}, u32[]{:S(2)}, u32[]{:S(2)}) collective-permute-start(bf16[320,2304]{1,0:T(8,128)(2,1)S(1)} %bitcast.101), channel_id=1, source_target_pairs={{0,8},{8,16},{16,24},{1,9},{9,17},{17,25},{2,10},{10,18},{18,26},{... | collective-permute-start | bytes 4423688 | tf_op jit(solution)/shard_map/ppermute | solution.py:16
  100.7 35.4 %collective-permute-start.7 = (bf16[320,2304]{1,0:T(8,128)(2,1)S(1)}, bf16[320,2304]{1,0:T(8,128)(2,1)S(1)}, u32[]{:S(2)}, u32[]{:S(2)}) collective-permute-start(bf16[320,2304]{1,0:T(8,128)(2,1)S(1)} %bitcast.102), channel_id=1, source_target_pairs={{8,0},{16,8},{24,16},{9,1},{17,9},{25,17},{10,2},{18,10},{26,18},{... | collective-permute-start | bytes 4423688 | tf_op jit(solution)/shard_map/ppermute | solution.py:20
  136.2 3.1 collective-permute-start.8
  138.0 36.9 %collective-permute-start.9 = (bf16[320,2304]{1,0:T(8,128)(2,1)S(1)}, bf16[320,2304]{1,0:T(8,128)(2,1)}, u32[]{:S(2)}, u32[]{:S(2)}) collective-permute-start(bf16[320,2304]{1,0:T(8,128)(2,1)S(1)} %collective-permute-done.7), channel_id=1, source_target_pairs={{8,0},{16,8},{9,1},{17,9},{10,2},{18,10},{11,3},{19,11},{12,4},{20... | collective-permute-start | bytes 4423688 | tf_op jit(solution)/shard_map/ppermute | solution.py:20
  174.9 3.1 collective-permute-start.10
  176.7 33.9 %collective-permute-start.11 = (bf16[320,2304]{1,0:T(8,128)(2,1)}, bf16[320,2304]{1,0:T(8,128)(2,1)}, u32[]{:S(2)}, u32[]{:S(2)}) collective-permute-start(bf16[320,2304]{1,0:T(8,128)(2,1)} %collective-permute-done.9), channel_id=1, source_target_pairs={{8,0},{9,1},{10,2},{11,3},{12,4},{13,5},{14,6},{15,7}} | collective-permute-start | bytes 4423688 | tf_op jit(solution)/shard_map/ppermute | solution.py:20
  235.9 36.9 %collective-permute-start.13 = (bf16[160,2304]{1,0:T(8,128)(2,1)}, bf16[160,2304]{1,0:T(8,128)(2,1)}, u32[]{:S(2)}, u32[]{:S(2)}) collective-permute-start(bf16[160,2304]{1,0:T(8,128)(2,1)} %fusion.28), channel_id=1, source_target_pairs={{0,8},{1,9},{2,10},{3,11},{4,12},{5,13},{6,14},{7,15}} | collective-permute-start | bytes 2211848 | tf_op jit(solution)/shard_map/ppermute | solution.py:16
  238.2 34.6 %collective-permute-start.17 = (bf16[160,2304]{1,0:T(8,128)(2,1)}, bf16[160,2304]{1,0:T(8,128)(2,1)}, u32[]{:S(2)}, u32[]{:S(2)}) collective-permute-start(bf16[160,2304]{1,0:T(8,128)(2,1)} %fusion.28), channel_id=1, source_target_pairs={{24,16},{25,17},{26,18},{27,19},{28,20},{29,21},{30,22},{31,23}} | collective-permute-start | bytes 2211848 | tf_op jit(solution)/shard_map/ppermute | solution.py:20
  245.0 27.8 %collective-permute-start.12 = (bf16[160,2304]{1,0:T(8,128)(2,1)}, bf16[160,2304]{1,0:T(8,128)(2,1)}, u32[]{:S(2)}, u32[]{:S(2)}) collective-permute-start(bf16[160,2304]{1,0:T(8,128)(2,1)} %fusion.25), channel_id=1, source_target_pairs={{0,8},{1,9},{2,10},{3,11},{4,12},{5,13},{6,14},{7,15}} | collective-permute-start | bytes 2211848 | tf_op jit(solution)/shard_map/ppermute | solution.py:16
  247.2 25.7 %collective-permute-start.16 = (bf16[160,2304]{1,0:T(8,128)(2,1)}, bf16[160,2304]{1,0:T(8,128)(2,1)}, u32[]{:S(2)}, u32[]{:S(2)}) collective-permute-start(bf16[160,2304]{1,0:T(8,128)(2,1)} %fusion.25), channel_id=1, source_target_pairs={{24,16},{25,17},{26,18},{27,19},{28,20},{29,21},{30,22},{31,23}} | collective-permute-start | bytes 2211848 | tf_op jit(solution)/shard_map/ppermute | solution.py:20
  280.7 29.7 %collective-permute-start.14 = (bf16[320,2304]{1,0:T(8,128)(2,1)S(1)}, bf16[320,2304]{1,0:T(8,128)(2,1)S(1)}, u32[]{:S(2)}, u32[]{:S(2)}) collective-permute-start(bf16[320,2304]{1,0:T(8,128)(2,1)S(1)} %get-tuple-element.19), channel_id=1, source_target_pairs={{0,8},{8,16},{1,9},{9,17},{2,10},{10,18},{3,11},{11,19},{4,12},{12... | collective-permute-start | bytes 4423688 | tf_op jit(solution)/shard_map/ppermute | solution.py:16
  282.1 28.3 %collective-permute-start.18 = (bf16[320,2304]{1,0:T(8,128)(2,1)S(1)}, bf16[320,2304]{1,0:T(8,128)(2,1)S(1)}, u32[]{:S(2)}, u32[]{:S(2)}) collective-permute-start(bf16[320,2304]{1,0:T(8,128)(2,1)S(1)} %get-tuple-element.20), channel_id=1, source_target_pairs={{16,8},{24,16},{17,9},{25,17},{18,10},{26,18},{19,11},{27,19},{20,... | collective-permute-start | bytes 4423688 | tf_op jit(solution)/shard_map/ppermute | solution.py:20
  311.2 32.6 %collective-permute-start.19 = (bf16[320,2304]{1,0:T(8,128)(2,1)S(1)}, bf16[320,2304]{1,0:T(8,128)(2,1)S(1)}, u32[]{:S(2)}, u32[]{:S(2)}) collective-permute-start(bf16[320,2304]{1,0:T(8,128)(2,1)S(1)} %get-tuple-element.18), channel_id=1, source_target_pairs={{8,0},{16,8},{24,16},{9,1},{17,9},{25,17},{10,2},{18,10},{26,18},{... | collective-permute-start | bytes 4423688 | tf_op jit(solution)/shard_map/ppermute | solution.py:20
  312.5 32.5 %collective-permute-start.15 = (bf16[320,2304]{1,0:T(8,128)(2,1)S(1)}, bf16[320,2304]{1,0:T(8,128)(2,1)S(1)}, u32[]{:S(2)}, u32[]{:S(2)}) collective-permute-start(bf16[320,2304]{1,0:T(8,128)(2,1)S(1)} %get-tuple-element.17), channel_id=1, source_target_pairs={{0,8},{8,16},{16,24},{1,9},{9,17},{17,25},{2,10},{10,18},{18,26},{... | collective-permute-start | bytes 4423688 | tf_op jit(solution)/shard_map/ppermute | solution.py:16
  346.8 23.6 %all-to-all-start.1 = ((bf16[8,40,2304]{2,1,0:T(8,128)(2,1)}), bf16[8,40,2304]{2,1,0:T(8,128)(2,1)S(1)}, u32[]{:S(2)}, u32[]{:S(2)}) async-start(bf16[8,40,2304]{2,1,0:T(8,128)(2,1)} %bitcast.95), calls=%async_computation.1 | async-start | bytes 2949120 | tf_op jit(solution)/shard_map/all_to_all | solution.py:163
  (14 other events, 152.3 us)

commit v2 on v0

--- a/solution.py
+++ b/solution.py
@@ -41,20 +41,19 @@
     query_seg = tenant[0]
     scale = HEAD_DIM ** (-0.5)
 
-    key_chunks = [keys[0]]
-    value_chunks = [values[0]]
-    seg_chunks = [tenant[0]]
-    k_cur, v_cur, s_cur = keys[0], values[0], tenant[0]
+    seg_cols = jnp.broadcast_to(tenant[0].astype(jnp.bfloat16)[:, None], (rows_here, 128))
+    k_cur = jnp.concatenate([keys[0], seg_cols], axis=1)
+    v_cur = values[0]
+    key_chunks, value_chunks = [k_cur], [v_cur]
     for _ in range(back):
         k_cur = shift_up(k_cur, 0, n_grp - 2)
         v_cur = shift_up(v_cur, 0, n_grp - 2)
-        s_cur = shift_up(s_cur, 0, n_grp - 2)
         key_chunks.insert(0, k_cur)
         value_chunks.insert(0, v_cur)
-        seg_chunks.insert(0, s_cur)
-    key_piece = jnp.concatenate(key_chunks, axis=0)
+    key_seg = jnp.concatenate(key_chunks, axis=0)
+    key_piece = key_seg[:, :width]
+    seg_piece = key_seg[:, width].astype(jnp.int32)
     value_piece = jnp.concatenate(value_chunks, axis=0)
-    seg_piece = jnp.concatenate(seg_chunks, axis=0)
     count = key_piece.shape[0]
     key_pos = offset - back * rows_here + jnp.arange(count, dtype=jnp.int32)
     key_heads = key_piece.reshape(count, HEADS, HEAD_DIM)

time: 353 us -> 363 us (1.028)
  waiting for transfers between devices: 170 us -> 184 us
  starting transfers between devices: 57.7 us -> 49.5 us
  matrix products: 81.1 us -> 86.8 us
    ppermute x12 -> x10, waiting for transfers between devices: 71.2 us -> 85.1 us  [shift_up(): lax.ppermute(x, 'grp', perm=[(i, i + 1) for i in range(first, last + 1)])]
    ppermute x12 -> x10, starting transfers between devices: 46.7 us -> 38.7 us  [shift_up(): lax.ppermute(x, 'grp', perm=[(i, i + 1) for i in range(first, last + 1)])]
    sub x0 -> x1, matrix products: none -> 6.88 us  [local(): probs = jnp.where(allowed[None], jnp.exp(scores - newest[..., None]), 0.0)]
    sub x1 -> x0, other arithmetic: 4.13 us -> none  [local(): probs = jnp.where(allowed[None], jnp.exp(scores - newest[..., None]), 0.0)]
  transfers between devices with their start and end apart: 19 -> 17, of which waited for: 12 -> 12; matrix products, arithmetic and copies ran while one was open for 19% -> 17% of each run, Pallas kernels for 0% -> 0%
where the time goes in v2:
time: 363 us; the launch traced here: 362 us
  waiting for transfers between devices  184 us (51%)
  matrix products  86.8 us (24%)
  starting transfers between devices  49.5 us (14%)
  blocking collectives  23.4 us (6%)
  local copies, waits for them, and re-layouts  9.62 us (3%)
  other arithmetic  8.35 us (2%)
    ppermute x10, waiting for transfers between devices, shift_up(): lax.ppermute(x, 'grp', perm=[(i, i + 1) for i in range(first, last + 1)])  85.1 us
    ppermute x6, waiting for transfers between devices, shift_down(): lax.ppermute(x, 'grp', perm=[(i, i - 1) for i in range(first, last + 1)])  79.2 us
    dot_general x4, matrix products, expert(): both = jnp.dot(rows, weight_matrix, preferred_element_type=jnp.float32)  44.6 us
    ppermute x10, starting transfers between devices, shift_up(): lax.ppermute(x, 'grp', perm=[(i, i + 1) for i in range(first, last + 1)])  38.7 us
    dot_general x4, matrix products, expert(): jnp.dot(hidden, weight_out, preferred_element_type=jnp.float32)  24.4 us
    all_to_all x1, blocking collectives, local(): lax.all_to_all(outgoing, 'ep', split_axis=0, concat_axis=0, tiled=True)  23.4 us
    all_to_all x1, waiting for transfers between devices, local(): lax.all_to_all(expert_output.reshape(n_ep, capacity, width), 'ep', split_...  19.5 us
  transfers between devices with their start and end apart: 17, of which 12 were waited for; matrix products, arithmetic and copies ran while one was open for 17% of the time, Pallas kernels for 0%

profile of v2, /device:TPU:0, one launch (start us, length us, event | category | flops | bytes accessed | tf_op | source)
XLA Modules:
  0.0 361.9 jit_solution(10124220205434013722)
XLA Ops:
  13.0 20.0 %collective-permute-done.2 = bf16[128,2304]{1,0:T(8,128)(2,1)S(1)} collective-permute-done((bf16[128,2304]{1,0:T(8,128)(2,1)}, bf16[128,2304]{1,0:T(8,128)(2,1)S(1)}, u32[]{:S(2)}, u32[]{:S(2)}) %collective-permute-start.2) | collective-permute-done | bytes 589856 | tf_op jit(solution)/shard_map/ppermute | solution.py:16
  45.0 6.0 %collective-permute-done.3 = bf16[128,2304]{1,0:T(8,128)(2,1)} collective-permute-done((bf16[128,2304]{1,0:T(8,128)(2,1)S(1)}, bf16[128,2304]{1,0:T(8,128)(2,1)}, u32[]{:S(2)}, u32[]{:S(2)}) %collective-permute-start.3) | collective-permute-done | bytes 589856 | tf_op jit(solution)/shard_map/ppermute | solution.py:16
  53.1 9.1 %collective-permute-done.1 = bf16[128,2432]{1,0:T(8,128)(2,1)} collective-permute-done((bf16[128,2432]{1,0:T(8,128)(2,1)S(1)}, bf16[128,2432]{1,0:T(8,128)(2,1)}, u32[]{:S(2)}, u32[]{:S(2)}) %collective-permute-start.1) | collective-permute-done | bytes 622624 | tf_op jit(solution)/shard_map/ppermute | solution.py:16
  66.9 6.9 %fusion.86 = (f32[36,128]{1,0:T(8,128)S(1)}, bf16[36,128,384]{1,2,0:T(8,128)(2,1)}) fusion(pred[128,384]{0,1:T(8,128)(4,1)S(1)} %compare_and_fusion, bf16[384,36,64]{0,2,1:T(8,128)(2,1)} %bitcast.86, bf16[128,36,64]{0,2,1:T(8,128)(2,1)} %bitcast.93), kind=kOutput, calls=%fused_computation.108 | convolution fusion | flops 237109632 | bytes 5965824 | tf_op jit(solution)/shard_map/sub | solution.py:72
  76.7 5.7 %multiply_reduce_fusion = (f32[128]{0:T(128)S(1)}, f32[128,2304]{1,0:T(8,128)S(1)}) fusion(bf16[128,2304]{0,1:T(8,128)(2,1)S(1)} %bitcast.90, bf16[2304,2304]{1,0:T(8,128)(2,1)} %param.16, bf16[1,128,2304]{2,1,0:T(8,128)(2,1)S(1)} %copy-done.7), kind=kOutput, calls=%fused_computation.62 | convolution fusion | flops 1360134016 | bytes 12976640 | tf_op jit(solution)/shard_map/dot_general | solution.py:82
  83.1 23.4 %all_to_all.10 = bf16[8,40,2304]{2,1,0:T(8,128)(2,1)S(1)} all-to-all(bf16[8,40,2304]{2,1,0:T(8,128)(2,1)S(1)} %bitcast.82), channel_id=1, replica_groups=mesh['grp'=4,'ep'=8] {'ep'}, dimensions={0} | all-to-all | bytes 2949120 | tf_op jit(solution)/shard_map/all_to_all | solution.py:124
  106.5 5.6 %collective-permute-start.4 = (bf16[320,2304]{1,0:T(8,128)(2,1)S(1)}, bf16[320,2304]{1,0:T(8,128)(2,1)}, u32[]{:S(2)}, u32[]{:S(2)}) collective-permute-start(bf16[320,2304]{1,0:T(8,128)(2,1)S(1)} %bitcast.87), channel_id=1, source_target_pairs={{0,8},{8,16},{16,24},{1,9},{9,17},{17,25},{2,10},{10,18},{18,26},{... | collective-permute-start | bytes 4423688 | tf_op jit(solution)/shard_map/ppermute | solution.py:16
  113.6 8.0 %fusion.87 = f32[320,2880]{1,0:T(8,128)S(1)} fusion(bf16[320,2304]{1,0:T(8,128)(2,1)S(1)} %bitcast.89, bf16[2304,2880]{0,1:T(8,128)(2,1)} %bitcast.98), kind=kOutput, calls=%fused_computation.109 | convolution fusion | flops 4246732800 | bytes 18432000 | tf_op jit(solution)/shard_map/dot_general | solution.py:120
  121.7 5.6 %fusion.13 = bf16[320,2304]{1,0:T(8,128)(2,1)S(1)} fusion(bf16[1,1440,2304]{2,1,0:T(8,128)(2,1)} %param.21, f32[320,2880]{1,0:T(8,128)S(1)} %fusion.87), kind=kOutput, calls=%fused_computation.13 | convolution fusion | flops 2126868480 | bytes 12042240 | tf_op jit(solution)/shard_map/dot_general | solution.py:122
  127.3 15.0 %collective-permute-done.4 = bf16[320,2304]{1,0:T(8,128)(2,1)} collective-permute-done((bf16[320,2304]{1,0:T(8,128)(2,1)S(1)}, bf16[320,2304]{1,0:T(8,128)(2,1)}, u32[]{:S(2)}, u32[]{:S(2)}) %collective-permute-start.4) | collective-permute-done | bytes 1474592 | tf_op jit(solution)/shard_map/ppermute | solution.py:16
  142.3 5.3 %collective-permute-done.5 = bf16[320,2304]{1,0:T(8,128)(2,1)} collective-permute-done((bf16[320,2304]{1,0:T(8,128)(2,1)S(1)}, bf16[320,2304]{1,0:T(8,128)(2,1)}, u32[]{:S(2)}, u32[]{:S(2)}) %collective-permute-start.5) | collective-permute-done | bytes 1474592 | tf_op jit(solution)/shard_map/ppermute | solution.py:20
  150.8 34.8 %collective-permute-done.7 = bf16[320,2304]{1,0:T(8,128)(2,1)} collective-permute-done((bf16[320,2304]{1,0:T(8,128)(2,1)}, bf16[320,2304]{1,0:T(8,128)(2,1)}, u32[]{:S(2)}, u32[]{:S(2)}) %collective-permute-start.7) | collective-permute-done | bytes 1474592 | tf_op jit(solution)/shard_map/ppermute | solution.py:20
  187.6 11.8 %fusion.49 = f32[320,2880]{1,0:T(8,128)} fusion(bf16[2304,2880]{0,1:T(8,128)(2,1)} %bitcast.99, bf16[320,2304]{1,0:T(8,128)(2,1)} %collective-permute-done.6, bf16[320,2304]{1,0:T(8,128)(2,1)} %collective-permute-done.7, pred[]{:T(512)S(6)} %ge.39), kind=kOutput, calls=%fused_computation.56 | convolution fusion | flops 4247470080 | bytes 19906560 | tf_op jit(solution)/shard_map/dot_general | solution.py:120
  199.4 6.8 %fusion.16 = bf16[320,2304]{1,0:T(8,128)(2,1)S(1)} fusion(bf16[1,1440,2304]{2,1,0:T(8,128)(2,1)} %param.21, f32[320,2880]{1,0:T(8,128)} %fusion.49), kind=kOutput, calls=%fused_computation.14 | convolution fusion | flops 2126868480 | bytes 12042240 | tf_op jit(solution)/shard_map/dot_general | solution.py:122
  206.3 13.8 %collective-permute-done.9 = bf16[320,2304]{1,0:T(8,128)(2,1)S(1)} collective-permute-done((bf16[320,2304]{1,0:T(8,128)(2,1)}, bf16[320,2304]{1,0:T(8,128)(2,1)S(1)}, u32[]{:S(2)}, u32[]{:S(2)}) %collective-permute-start.9) | collective-permute-done | bytes 1474592 | tf_op jit(solution)/shard_map/ppermute | solution.py:20
  220.1 10.2 %fusion.47 = f32[320,2880]{1,0:T(8,128)} fusion(bf16[2304,2880]{0,1:T(8,128)(2,1)} %bitcast.100, bf16[320,2304]{1,0:T(8,128)(2,1)S(1)} %collective-permute-done.8, bf16[320,2304]{1,0:T(8,128)(2,1)S(1)} %collective-permute-done.9, pred[]{:T(512)S(6)} %ge.40), kind=kOutput, calls=%fused_computation.54 | convolution fusion | flops 4247470080 | bytes 19906560 | tf_op jit(solution)/shard_map/dot_general | solution.py:120
  230.3 6.8 %fusion.19 = bf16[320,2304]{1,0:T(8,128)(2,1)S(1)} fusion(bf16[1,1440,2304]{2,1,0:T(8,128)(2,1)} %param.21, f32[320,2880]{1,0:T(8,128)} %fusion.47), kind=kOutput, calls=%fused_computation.15 | convolution fusion | flops 2126868480 | bytes 12042240 | tf_op jit(solution)/shard_map/dot_general | solution.py:122
  239.5 27.4 %collective-permute-done.10 = bf16[320,2304]{1,0:T(8,128)(2,1)S(1)} collective-permute-done((bf16[320,2304]{1,0:T(8,128)(2,1)S(1)}, bf16[320,2304]{1,0:T(8,128)(2,1)S(1)}, u32[]{:S(2)}, u32[]{:S(2)}) %collective-permute-start.10) | collective-permute-done | bytes 1474592 | tf_op jit(solution)/shard_map/ppermute | solution.py:16
  273.3 14.6 %fusion.32 = f32[640,2880]{0,1:T(8,128)S(1)} fusion(bf16[2304,2880]{0,1:T(8,128)(2,1)} %bitcast.101, bf16[320,2304]{1,0:T(8,128)(2,1)} %collective-permute-done.5, bf16[320,2304]{1,0:T(8,128)(2,1)} %collective-permute-done.4), kind=kOutput, calls=%fused_computation.32 | convolution fusion | flops 8499363840 | bytes 23592960 | tf_op jit(solution)/shard_map/dot_general | solution.py:120
  287.9 5.2 %fusion.10 = bf16[640,2304]{1,0:T(8,128)(2,1)S(1)} fusion(bf16[1,1440,2304]{2,1,0:T(8,128)(2,1)S(1)} %bitcast.103, f32[640,2880]{0,1:T(8,128)S(1)} %fusion.32), kind=kOutput, calls=%fused_computation.12 | convolution fusion | flops 4253736960 | bytes 16957440 | tf_op jit(solution)/shard_map/dot_general | solution.py:122
  293.1 6.3 %collective-permute-done.11 = bf16[320,2304]{1,0:T(8,128)(2,1)S(1)} collective-permute-done((bf16[320,2304]{1,0:T(8,128)(2,1)S(1)}, bf16[320,2304]{1,0:T(8,128)(2,1)S(1)}, u32[]{:S(2)}, u32[]{:S(2)}) %collective-permute-start.11) | collective-permute-done | bytes 1474592 | tf_op jit(solution)/shard_map/ppermute | solution.py:16
  301.6 7.3 %collective-permute-start.12 = (bf16[320,2304]{1,0:T(8,128)(2,1)S(1)}, bf16[320,2304]{1,0:T(8,128)(2,1)S(1)}, u32[]{:S(2)}, u32[]{:S(2)}) collective-permute-start(bf16[320,2304]{1,0:T(8,128)(2,1)S(1)} %get-tuple-element.21), channel_id=1, source_target_pairs={{0,8},{8,16},{16,24},{1,9},{9,17},{17,25},{2,10},{10,18},{18,26},{... | collective-permute-start | bytes 4423688 | tf_op jit(solution)/shard_map/ppermute | solution.py:16
  308.9 25.2 %collective-permute-done.15 = bf16[320,2304]{1,0:T(8,128)(2,1)S(1)} collective-permute-done((bf16[320,2304]{1,0:T(8,128)(2,1)S(1)}, bf16[320,2304]{1,0:T(8,128)(2,1)S(1)}, u32[]{:S(2)}, u32[]{:S(2)}) %collective-permute-start.15) | collective-permute-done | bytes 1474592 | tf_op jit(solution)/shard_map/ppermute | solution.py:20
  341.1 19.5 %all-to-all-done.1 = bf16[8,40,2304]{2,1,0:T(8,128)(2,1)S(1)} async-done(((bf16[8,40,2304]{2,1,0:T(8,128)(2,1)}), bf16[8,40,2304]{2,1,0:T(8,128)(2,1)S(1)}, u32[]{:S(2)}, u32[]{:S(2)}) %all-to-all-start.1) | async-done | bytes 1474592 | tf_op jit(solution)/shard_map/all_to_all | solution.py:160
  (96 shorter events, 60.9 us)
Async XLA Ops:
  0.0 340.6 %copy-start = (bf16[2304,8]{0,1:T(8,128)(2,1)S(1)}, bf16[2304,8]{0,1:T(8,128)(2,1)}, u32[]{:S(2)}) copy-start(bf16[2304,8]{0,1:T(8,128)(2,1)} %param.18) | copy-start | bytes 110596
  0.0 41.5 %copy-start.2 = (bf16[1,128,2304]{2,1,0:T(8,128)(2,1)S(1)}, bf16[1,128,2304]{2,1,0:T(8,128)(2,1)}, u32[]{:S(2)}) copy-start(bf16[1,128,2304]{2,1,0:T(8,128)(2,1)} %param.14) | copy-start | bytes 1769476
  0.0 42.6 %copy-start.3 = (bf16[1,128,2304]{2,1,0:T(8,128)(2,1)S(1)}, bf16[1,128,2304]{2,1,0:T(8,128)(2,1)}, u32[]{:S(2)}) copy-start(bf16[1,128,2304]{2,1,0:T(8,128)(2,1)} %param.12) | copy-start | bytes 1769476
  0.9 43.1 %copy-start.9 = (s32[1,128,2]{1,2,0:T(2,128)S(1)}, s32[1,128,2]{1,2,0:T(2,128)}, u32[]{:S(2)}) copy-start(s32[1,128,2]{1,2,0:T(2,128)} %param.19) | copy-start | bytes 3076
  2.0 36.0 %collective-permute-start = (bf16[128,2432]{1,0:T(8,128)(2,1)S(1)}, bf16[128,2432]{1,0:T(8,128)(2,1)S(1)}, u32[]{:S(2)}, u32[]{:S(2)}) collective-permute-start(bf16[128,2432]{1,0:T(8,128)(2,1)S(1)} %pad_maximum_fusion.2), channel_id=1, source_target_pairs={{0,8},{8,16},{16,24},{1,9},{9,17},{17,25},{2,10},{10,18},{18,26},{... | collective-permute-start | bytes 1867784 | tf_op jit(solution)/shard_map/ppermute | solution.py:16
  7.0 26.0 %collective-permute-start.2 = (bf16[128,2304]{1,0:T(8,128)(2,1)}, bf16[128,2304]{1,0:T(8,128)(2,1)S(1)}, u32[]{:S(2)}, u32[]{:S(2)}) collective-permute-start(bf16[128,2304]{1,0:T(8,128)(2,1)} %bitcast.91), channel_id=1, source_target_pairs={{0,8},{8,16},{16,24},{1,9},{9,17},{17,25},{2,10},{10,18},{18,26},{... | collective-permute-start | bytes 1769480 | tf_op jit(solution)/shard_map/ppermute | solution.py:16
  32.9 18.0 %collective-permute-start.3 = (bf16[128,2304]{1,0:T(8,128)(2,1)S(1)}, bf16[128,2304]{1,0:T(8,128)(2,1)}, u32[]{:S(2)}, u32[]{:S(2)}) collective-permute-start(bf16[128,2304]{1,0:T(8,128)(2,1)S(1)} %collective-permute-done.2), channel_id=1, source_target_pairs={{0,8},{8,16},{16,24},{1,9},{9,17},{17,25},{2,10},{10,18},{18,26},{... | collective-permute-start | bytes 1769480 | tf_op jit(solution)/shard_map/ppermute | solution.py:16
  38.0 24.2 %collective-permute-start.1 = (bf16[128,2432]{1,0:T(8,128)(2,1)S(1)}, bf16[128,2432]{1,0:T(8,128)(2,1)}, u32[]{:S(2)}, u32[]{:S(2)}) collective-permute-start(bf16[128,2432]{1,0:T(8,128)(2,1)S(1)} %collective-permute-done), channel_id=1, source_target_pairs={{0,8},{8,16},{16,24},{1,9},{9,17},{17,25},{2,10},{10,18},{18,26},{... | collective-permute-start | bytes 1867784 | tf_op jit(solution)/shard_map/ppermute | solution.py:16
  42.6 19.6 %copy-start.1 = (bf16[1,128,2304]{2,1,0:T(8,128)(2,1)S(1)}, bf16[1,128,2304]{2,1,0:T(8,128)(2,1)}, u32[]{:S(2)}) copy-start(bf16[1,128,2304]{2,1,0:T(8,128)(2,1)} %param.13) | copy-start | bytes 1769476
  106.5 35.8 %collective-permute-start.4 = (bf16[320,2304]{1,0:T(8,128)(2,1)S(1)}, bf16[320,2304]{1,0:T(8,128)(2,1)}, u32[]{:S(2)}, u32[]{:S(2)}) collective-permute-start(bf16[320,2304]{1,0:T(8,128)(2,1)S(1)} %bitcast.87), channel_id=1, source_target_pairs={{0,8},{8,16},{16,24},{1,9},{9,17},{17,25},{2,10},{10,18},{18,26},{... | collective-permute-start | bytes 4423688 | tf_op jit(solution)/shard_map/ppermute | solution.py:16
  112.1 35.5 %collective-permute-start.5 = (bf16[320,2304]{1,0:T(8,128)(2,1)S(1)}, bf16[320,2304]{1,0:T(8,128)(2,1)}, u32[]{:S(2)}, u32[]{:S(2)}) collective-permute-start(bf16[320,2304]{1,0:T(8,128)(2,1)S(1)} %bitcast.88), channel_id=1, source_target_pairs={{8,0},{16,8},{24,16},{9,1},{17,9},{25,17},{10,2},{18,10},{26,18},{... | collective-permute-start | bytes 4423688 | tf_op jit(solution)/shard_map/ppermute | solution.py:20
  147.7 3.1 collective-permute-start.6
  149.5 36.1 %collective-permute-start.7 = (bf16[320,2304]{1,0:T(8,128)(2,1)}, bf16[320,2304]{1,0:T(8,128)(2,1)}, u32[]{:S(2)}, u32[]{:S(2)}) collective-permute-start(bf16[320,2304]{1,0:T(8,128)(2,1)} %collective-permute-done.5), channel_id=1, source_target_pairs={{8,0},{16,8},{9,1},{17,9},{10,2},{18,10},{11,3},{19,11},{12,4},{20... | collective-permute-start | bytes 4423688 | tf_op jit(solution)/shard_map/ppermute | solution.py:20
  185.6 20.7 %collective-permute-start.8 = (bf16[320,2304]{1,0:T(8,128)(2,1)}, bf16[320,2304]{1,0:T(8,128)(2,1)S(1)}, u32[]{:S(2)}, u32[]{:S(2)}) collective-permute-start(bf16[320,2304]{1,0:T(8,128)(2,1)} %collective-permute-done.6), channel_id=1, source_target_pairs={{16,24},{17,25},{18,26},{19,27},{20,28},{21,29},{22,30},{23,31}} | collective-permute-start | bytes 4423688 | tf_op jit(solution)/shard_map/ppermute | solution.py:16
  186.3 33.8 %collective-permute-start.9 = (bf16[320,2304]{1,0:T(8,128)(2,1)}, bf16[320,2304]{1,0:T(8,128)(2,1)S(1)}, u32[]{:S(2)}, u32[]{:S(2)}) collective-permute-start(bf16[320,2304]{1,0:T(8,128)(2,1)} %collective-permute-done.7), channel_id=1, source_target_pairs={{8,0},{9,1},{10,2},{11,3},{12,4},{13,5},{14,6},{15,7}} | collective-permute-start | bytes 4423688 | tf_op jit(solution)/shard_map/ppermute | solution.py:20
  237.1 29.9 %collective-permute-start.10 = (bf16[320,2304]{1,0:T(8,128)(2,1)S(1)}, bf16[320,2304]{1,0:T(8,128)(2,1)S(1)}, u32[]{:S(2)}, u32[]{:S(2)}) collective-permute-start(bf16[320,2304]{1,0:T(8,128)(2,1)S(1)} %fusion.19), channel_id=1, source_target_pairs={{0,8},{1,9},{2,10},{3,11},{4,12},{5,13},{6,14},{7,15}} | collective-permute-start | bytes 4423688 | tf_op jit(solution)/shard_map/ppermute | solution.py:16
  238.8 28.2 %collective-permute-start.13 = (bf16[320,2304]{1,0:T(8,128)(2,1)S(1)}, bf16[320,2304]{1,0:T(8,128)(2,1)S(1)}, u32[]{:S(2)}, u32[]{:S(2)}) collective-permute-start(bf16[320,2304]{1,0:T(8,128)(2,1)S(1)} %fusion.19), channel_id=1, source_target_pairs={{24,16},{25,17},{26,18},{27,19},{28,20},{29,21},{30,22},{31,23}} | collective-permute-start | bytes 4423688 | tf_op jit(solution)/shard_map/ppermute | solution.py:20
  267.7 31.8 %collective-permute-start.11 = (bf16[320,2304]{1,0:T(8,128)(2,1)S(1)}, bf16[320,2304]{1,0:T(8,128)(2,1)S(1)}, u32[]{:S(2)}, u32[]{:S(2)}) collective-permute-start(bf16[320,2304]{1,0:T(8,128)(2,1)S(1)} %get-tuple-element.23), channel_id=1, source_target_pairs={{0,8},{8,16},{1,9},{9,17},{2,10},{10,18},{3,11},{11,19},{4,12},{12... | collective-permute-start | bytes 4423688 | tf_op jit(solution)/shard_map/ppermute | solution.py:16
  272.2 15.7 %slice-start = ((s8[6635520]{0:T(1024)(128)(4,1)}), s8[4194304]{0:T(1024)(128)(4,1)S(1)}, s32[]{:S(2)}) async-start(s8[6635520]{0:T(1024)(128)(4,1)} %bitcast.102), calls=%async_computation.2 | async-start | bytes 8388608
  272.2 15.7 %slice-start.1 = ((s8[6635520]{0:T(1024)(128)(4,1)}), s8[2441216]{0:T(1024)(128)(4,1)S(1)}, s32[]{:S(2)}) async-start(s8[6635520]{0:T(1024)(128)(4,1)} %bitcast.102), calls=%async_computation.3 | async-start | bytes 4882432
  272.2 27.3 %collective-permute-start.14 = (bf16[320,2304]{1,0:T(8,128)(2,1)S(1)}, bf16[320,2304]{1,0:T(8,128)(2,1)S(1)}, u32[]{:S(2)}, u32[]{:S(2)}) collective-permute-start(bf16[320,2304]{1,0:T(8,128)(2,1)S(1)} %get-tuple-element.24), channel_id=1, source_target_pairs={{16,8},{24,16},{17,9},{25,17},{18,10},{26,18},{19,11},{27,19},{20,... | collective-permute-start | bytes 4423688 | tf_op jit(solution)/shard_map/ppermute | solution.py:20
  300.3 33.8 %collective-permute-start.15 = (bf16[320,2304]{1,0:T(8,128)(2,1)S(1)}, bf16[320,2304]{1,0:T(8,128)(2,1)S(1)}, u32[]{:S(2)}, u32[]{:S(2)}) collective-permute-start(bf16[320,2304]{1,0:T(8,128)(2,1)S(1)} %get-tuple-element.22), channel_id=1, source_target_pairs={{8,0},{16,8},{24,16},{9,1},{17,9},{25,17},{10,2},{18,10},{26,18},{... | collective-permute-start | bytes 4423688 | tf_op jit(solution)/shard_map/ppermute | solution.py:20
  301.6 33.7 %collective-permute-start.12 = (bf16[320,2304]{1,0:T(8,128)(2,1)S(1)}, bf16[320,2304]{1,0:T(8,128)(2,1)S(1)}, u32[]{:S(2)}, u32[]{:S(2)}) collective-permute-start(bf16[320,2304]{1,0:T(8,128)(2,1)S(1)} %get-tuple-element.21), channel_id=1, source_target_pairs={{0,8},{8,16},{16,24},{1,9},{9,17},{17,25},{2,10},{10,18},{18,26},{... | collective-permute-start | bytes 4423688 | tf_op jit(solution)/shard_map/ppermute | solution.py:16
  337.0 23.6 %all-to-all-start.1 = ((bf16[8,40,2304]{2,1,0:T(8,128)(2,1)}), bf16[8,40,2304]{2,1,0:T(8,128)(2,1)S(1)}, u32[]{:S(2)}, u32[]{:S(2)}) async-start(bf16[8,40,2304]{2,1,0:T(8,128)(2,1)} %bitcast.81), calls=%async_computation.1 | async-start | bytes 2949120 | tf_op jit(solution)/shard_map/all_to_all | solution.py:160
  (6 other events, 32.6 us)

commit v3 on v0

--- a/solution.py
+++ b/solution.py
@@ -52,29 +52,36 @@
         key_chunks.insert(0, k_cur)
         value_chunks.insert(0, v_cur)
         seg_chunks.insert(0, s_cur)
-    key_piece = jnp.concatenate(key_chunks, axis=0)
-    value_piece = jnp.concatenate(value_chunks, axis=0)
-    seg_piece = jnp.concatenate(seg_chunks, axis=0)
-    count = key_piece.shape[0]
-    key_pos = offset - back * rows_here + jnp.arange(count, dtype=jnp.int32)
-    key_heads = key_piece.reshape(count, HEADS, HEAD_DIM)
-    value_heads = value_piece.reshape(count, HEADS, HEAD_DIM)
-    scores = (
-        jnp.einsum("qhd,khd->hqk", query_heads, key_heads, preferred_element_type=jnp.float32)
-        * scale
-    )
-    allowed = (
-        (query_pos[:, None] >= key_pos[None, :])
-        & (key_pos[None, :] >= 0)
-        & (query_seg[:, None] == seg_piece[None, :])
-    )
-    scores = jnp.where(allowed[None], scores, NEG)
-    newest = jnp.max(scores, axis=-1)
-    probs = jnp.where(allowed[None], jnp.exp(scores - newest[..., None]), 0.0)
-    total = jnp.sum(probs, axis=-1)
-    accum = jnp.einsum(
-        "hqk,khd->hqd", probs.astype(jnp.bfloat16), value_heads, preferred_element_type=jnp.float32
-    )
+    scores, allowed = [], []
+    for j in range(back + 1):
+        key_pos = offset + (j - back) * rows_here + jnp.arange(rows_here, dtype=jnp.int32)
+        key_heads = key_chunks[j].reshape(rows_here, HEADS, HEAD_DIM)
+        kept = (
+            (query_pos[:, None] >= key_pos[None, :])
+            & (key_pos[None, :] >= 0)
+            & (query_seg[:, None] == seg_chunks[j][None, :])
+        )
+        raw = (
+            jnp.einsum("qhd,khd->hqk", query_heads, key_heads, preferred_element_type=jnp.float32)
+            * scale
+        )
+        scores.append(jnp.where(kept[None], raw, NEG))
+        allowed.append(kept)
+    newest = scores[0].max(axis=-1)
+    for part in scores[1:]:
+        newest = jnp.maximum(newest, part.max(axis=-1))
+    total = 0.0
+    accum = 0.0
+    for j in range(back + 1):
+        probs = jnp.where(allowed[j][None], jnp.exp(scores[j] - newest[..., None]), 0.0)
+        total = total + jnp.sum(probs, axis=-1)
+        value_heads = value_chunks[j].reshape(rows_here, HEADS, HEAD_DIM)
+        accum = accum + jnp.einsum(
+            "hqk,khd->hqd",
+            probs.astype(jnp.bfloat16),
+            value_heads,
+            preferred_element_type=jnp.float32,
+        )
     attended = (
         jnp.transpose(accum / total[..., None], (1, 0, 2))
         .reshape(rows_here, width)

time: 353 us -> 352 us (level)
  waiting for transfers between devices: 170 us -> 161 us
  matrix products: 81.1 us -> 89.8 us
  local copies, waits for them, and re-layouts: 9.86 us -> 14.3 us
    ppermute x12, waiting for transfers between devices: 71.2 us -> 63 us  [shift_up(): lax.ppermute(x, 'grp', perm=[(i, i + 1) for i in range(first, last + 1)])]
    dot_general x1 -> x3, matrix products: 1.14 us -> 6.57 us  [local(): jnp.einsum('qhd,khd->hqk', query_heads, key_heads, preferred_element_type...]
    sub x1 -> x0, other arithmetic: 4.13 us -> none  [local(): probs = jnp.where(allowed[None], jnp.exp(scores - newest[..., None]), 0.0)]
  transfers between devices with their start and end apart: 19 -> 19, of which waited for: 12 -> 12; matrix products, arithmetic and copies ran while one was open for 19% -> 23% of each run, Pallas kernels for 0% -> 0%
where the time goes in v3:
time: 352 us; the launch traced here: 351 us
  waiting for transfers between devices  161 us (46%)
  matrix products  89.8 us (26%)
  starting transfers between devices  55.4 us (16%)
  blocking collectives  23.4 us (7%)
  local copies, waits for them, and re-layouts  14.3 us (4%)
  other arithmetic  7.04 us (2%)
    ppermute x6, waiting for transfers between devices, shift_down(): lax.ppermute(x, 'grp', perm=[(i, i - 1) for i in range(first, last + 1)])  78.2 us
    ppermute x12, waiting for transfers between devices, shift_up(): lax.ppermute(x, 'grp', perm=[(i, i + 1) for i in range(first, last + 1)])  63 us
    dot_general x4, matrix products, expert(): both = jnp.dot(rows, weight_matrix, preferred_element_type=jnp.float32)  44.6 us
    ppermute x12, starting transfers between devices, shift_up(): lax.ppermute(x, 'grp', perm=[(i, i + 1) for i in range(first, last + 1)])  44.4 us
    dot_general x4, matrix products, expert(): jnp.dot(hidden, weight_out, preferred_element_type=jnp.float32)  24.4 us
    all_to_all x1, blocking collectives, local(): lax.all_to_all(outgoing, 'ep', split_axis=0, concat_axis=0, tiled=True)  23.4 us
    all_to_all x1, waiting for transfers between devices, local(): lax.all_to_all(expert_output.reshape(n_ep, capacity, width), 'ep', split_...  19.5 us
    ppermute x4, local copies, waits for them, and re-layouts, shift_up(): lax.ppermute(x, 'grp', perm=[(i, i + 1) for i in range(first, last + 1)])  7.72 us
  transfers between devices with their start and end apart: 19, of which 12 were waited for; matrix products, arithmetic and copies ran while one was open for 23% of the time, Pallas kernels for 0%

profile of v3, /device:TPU:0, one launch (start us, length us, event | category | flops | bytes accessed | tf_op | source)
XLA Modules:
  0.0 351.1 jit_solution(1048651761295555385)
XLA Ops:
  0.0 5.1 %collective-permute-start = (s32[128]{0:T(128)}, s32[128]{0:T(128)S(1)}, u32[]{:S(2)}, u32[]{:S(2)}) collective-permute-start(s32[128]{0:T(128)} %bitcast.96), channel_id=1, source_target_pairs={{0,8},{8,16},{16,24},{1,9},{9,17},{17,25},{2,10},{10,18},{18,26},{... | collective-permute-start | bytes 1544 | tf_op jit(solution)/shard_map/ppermute | solution.py:16
  22.3 11.5 %collective-permute-done.1 = s32[128]{0:T(128)S(1)} collective-permute-done((s32[128]{0:T(128)S(1)}, s32[128]{0:T(128)S(1)}, u32[]{:S(2)}, u32[]{:S(2)}) %collective-permute-start.1) | collective-permute-done | bytes 544 | tf_op jit(solution)/shard_map/ppermute | solution.py:16
  34.1 5.2 %collective-permute-start.3 = (bf16[128,2304]{1,0:T(8,128)(2,1)}, bf16[128,2304]{1,0:T(8,128)(2,1)}, u32[]{:S(2)}, u32[]{:S(2)}) collective-permute-start(bf16[128,2304]{1,0:T(8,128)(2,1)} %collective-permute-done.2), channel_id=1, source_target_pairs={{0,8},{8,16},{16,24},{1,9},{9,17},{17,25},{2,10},{10,18},{18,26},{... | collective-permute-start | bytes 1769480 | tf_op jit(solution)/shard_map/ppermute | solution.py:16
  66.8 5.7 %multiply_reduce_fusion = (f32[128]{0:T(128)S(1)}, f32[128,2304]{1,0:T(8,128)S(1)}) fusion(bf16[128,2304]{0,1:T(8,128)(2,1)S(1)} %bitcast.89, bf16[2304,2304]{1,0:T(8,128)(2,1)} %param.16, bf16[1,128,2304]{2,1,0:T(8,128)(2,1)S(1)} %copy-done.7), kind=kOutput, calls=%fused_computation.66 | convolution fusion | flops 1360134016 | bytes 12976640 | tf_op jit(solution)/shard_map/dot_general | solution.py:90
  73.2 23.4 %all_to_all.10 = bf16[8,40,2304]{2,1,0:T(8,128)(2,1)S(1)} all-to-all(bf16[8,40,2304]{2,1,0:T(8,128)(2,1)S(1)} %bitcast.82), channel_id=1, replica_groups=mesh['grp'=4,'ep'=8] {'ep'}, dimensions={0} | all-to-all | bytes 2949120 | tf_op jit(solution)/shard_map/all_to_all | solution.py:132
  96.6 5.5 %collective-permute-start.6 = (bf16[320,2304]{1,0:T(8,128)(2,1)S(1)}, bf16[320,2304]{1,0:T(8,128)(2,1)}, u32[]{:S(2)}, u32[]{:S(2)}) collective-permute-start(bf16[320,2304]{1,0:T(8,128)(2,1)S(1)} %bitcast.86), channel_id=1, source_target_pairs={{0,8},{8,16},{16,24},{1,9},{9,17},{17,25},{2,10},{10,18},{18,26},{... | collective-permute-start | bytes 4423688 | tf_op jit(solution)/shard_map/ppermute | solution.py:16
  103.6 8.0 %fusion.101 = f32[320,2880]{1,0:T(8,128)S(1)} fusion(bf16[320,2304]{1,0:T(8,128)(2,1)S(1)} %bitcast.88, bf16[2304,2880]{0,1:T(8,128)(2,1)} %bitcast.98), kind=kOutput, calls=%fused_computation.135 | convolution fusion | flops 4246732800 | bytes 18432000 | tf_op jit(solution)/shard_map/dot_general | solution.py:128
  111.6 5.6 %fusion.11 = bf16[320,2304]{1,0:T(8,128)(2,1)S(1)} fusion(bf16[1,1440,2304]{2,1,0:T(8,128)(2,1)} %param.21, f32[320,2880]{1,0:T(8,128)S(1)} %fusion.101), kind=kOutput, calls=%fused_computation.9 | convolution fusion | flops 2126868480 | bytes 12042240 | tf_op jit(solution)/shard_map/dot_general | solution.py:130
  117.3 15.0 %collective-permute-done.6 = bf16[320,2304]{1,0:T(8,128)(2,1)} collective-permute-done((bf16[320,2304]{1,0:T(8,128)(2,1)S(1)}, bf16[320,2304]{1,0:T(8,128)(2,1)}, u32[]{:S(2)}, u32[]{:S(2)}) %collective-permute-start.6) | collective-permute-done | bytes 1474592 | tf_op jit(solution)/shard_map/ppermute | solution.py:16
  132.3 5.3 %collective-permute-done.7 = bf16[320,2304]{1,0:T(8,128)(2,1)} collective-permute-done((bf16[320,2304]{1,0:T(8,128)(2,1)S(1)}, bf16[320,2304]{1,0:T(8,128)(2,1)}, u32[]{:S(2)}, u32[]{:S(2)}) %collective-permute-start.7) | collective-permute-done | bytes 1474592 | tf_op jit(solution)/shard_map/ppermute | solution.py:20
  140.7 33.8 %collective-permute-done.9 = bf16[320,2304]{1,0:T(8,128)(2,1)} collective-permute-done((bf16[320,2304]{1,0:T(8,128)(2,1)}, bf16[320,2304]{1,0:T(8,128)(2,1)}, u32[]{:S(2)}, u32[]{:S(2)}) %collective-permute-start.9) | collective-permute-done | bytes 1474592 | tf_op jit(solution)/shard_map/ppermute | solution.py:20
  176.6 11.8 %fusion.45 = f32[320,2880]{1,0:T(8,128)} fusion(bf16[2304,2880]{0,1:T(8,128)(2,1)} %bitcast.99, bf16[320,2304]{1,0:T(8,128)(2,1)} %collective-permute-done.8, bf16[320,2304]{1,0:T(8,128)(2,1)} %collective-permute-done.9, pred[]{:T(512)S(6)} %ge.87), kind=kOutput, calls=%fused_computation.54 | convolution fusion | flops 4247470080 | bytes 19906560 | tf_op jit(solution)/shard_map/dot_general | solution.py:128
  188.4 6.8 %fusion.14 = bf16[320,2304]{1,0:T(8,128)(2,1)S(1)} fusion(bf16[1,1440,2304]{2,1,0:T(8,128)(2,1)} %param.21, f32[320,2880]{1,0:T(8,128)} %fusion.45), kind=kOutput, calls=%fused_computation.10 | convolution fusion | flops 2126868480 | bytes 12042240 | tf_op jit(solution)/shard_map/dot_general | solution.py:130
  195.3 13.9 %collective-permute-done.11 = bf16[320,2304]{1,0:T(8,128)(2,1)S(1)} collective-permute-done((bf16[320,2304]{1,0:T(8,128)(2,1)}, bf16[320,2304]{1,0:T(8,128)(2,1)S(1)}, u32[]{:S(2)}, u32[]{:S(2)}) %collective-permute-start.11) | collective-permute-done | bytes 1474592 | tf_op jit(solution)/shard_map/ppermute | solution.py:20
  209.1 10.2 %fusion.43 = f32[320,2880]{1,0:T(8,128)} fusion(bf16[2304,2880]{0,1:T(8,128)(2,1)} %bitcast.100, bf16[320,2304]{1,0:T(8,128)(2,1)S(1)} %collective-permute-done.10, bf16[320,2304]{1,0:T(8,128)(2,1)S(1)} %collective-permute-done.11, pred[]{:T(512)S(6)} %ge.88), kind=kOutput, calls=%fused_computation.52 | convolution fusion | flops 4247470080 | bytes 19906560 | tf_op jit(solution)/shard_map/dot_general | solution.py:128
  219.3 6.8 %fusion.17 = bf16[320,2304]{1,0:T(8,128)(2,1)S(1)} fusion(bf16[1,1440,2304]{2,1,0:T(8,128)(2,1)} %param.21, f32[320,2880]{1,0:T(8,128)} %fusion.43), kind=kOutput, calls=%fused_computation.11 | convolution fusion | flops 2126868480 | bytes 12042240 | tf_op jit(solution)/shard_map/dot_general | solution.py:130
  228.6 27.4 %collective-permute-done.12 = bf16[320,2304]{1,0:T(8,128)(2,1)S(1)} collective-permute-done((bf16[320,2304]{1,0:T(8,128)(2,1)S(1)}, bf16[320,2304]{1,0:T(8,128)(2,1)S(1)}, u32[]{:S(2)}, u32[]{:S(2)}) %collective-permute-start.12) | collective-permute-done | bytes 1474592 | tf_op jit(solution)/shard_map/ppermute | solution.py:16
  256.7 4.5 %collective-permute-start.13 = (bf16[320,2304]{1,0:T(8,128)(2,1)S(1)}, bf16[320,2304]{1,0:T(8,128)(2,1)S(1)}, u32[]{:S(2)}, u32[]{:S(2)}) collective-permute-start(bf16[320,2304]{1,0:T(8,128)(2,1)S(1)} %get-tuple-element.26), channel_id=1, source_target_pairs={{0,8},{8,16},{1,9},{9,17},{2,10},{10,18},{3,11},{11,19},{4,12},{12... | collective-permute-start | bytes 4423688 | tf_op jit(solution)/shard_map/ppermute | solution.py:16
  262.3 14.6 %fusion.25 = f32[640,2880]{0,1:T(8,128)S(1)} fusion(bf16[2304,2880]{0,1:T(8,128)(2,1)} %bitcast.101, bf16[320,2304]{1,0:T(8,128)(2,1)} %collective-permute-done.7, bf16[320,2304]{1,0:T(8,128)(2,1)} %collective-permute-done.6), kind=kOutput, calls=%fused_computation.23 | convolution fusion | flops 8499363840 | bytes 23592960 | tf_op jit(solution)/shard_map/dot_general | solution.py:128
  277.0 5.2 %fusion.8 = bf16[640,2304]{1,0:T(8,128)(2,1)S(1)} fusion(bf16[1,1440,2304]{2,1,0:T(8,128)(2,1)S(1)} %bitcast.103, f32[640,2880]{0,1:T(8,128)S(1)} %fusion.25), kind=kOutput, calls=%fused_computation.8 | convolution fusion | flops 4253736960 | bytes 16957440 | tf_op jit(solution)/shard_map/dot_general | solution.py:130
  282.1 6.3 %collective-permute-done.13 = bf16[320,2304]{1,0:T(8,128)(2,1)S(1)} collective-permute-done((bf16[320,2304]{1,0:T(8,128)(2,1)S(1)}, bf16[320,2304]{1,0:T(8,128)(2,1)S(1)}, u32[]{:S(2)}, u32[]{:S(2)}) %collective-permute-start.13) | collective-permute-done | bytes 1474592 | tf_op jit(solution)/shard_map/ppermute | solution.py:16
  290.6 7.3 %collective-permute-start.14 = (bf16[320,2304]{1,0:T(8,128)(2,1)S(1)}, bf16[320,2304]{1,0:T(8,128)(2,1)S(1)}, u32[]{:S(2)}, u32[]{:S(2)}) collective-permute-start(bf16[320,2304]{1,0:T(8,128)(2,1)S(1)} %get-tuple-element.24), channel_id=1, source_target_pairs={{0,8},{8,16},{16,24},{1,9},{9,17},{17,25},{2,10},{10,18},{18,26},{... | collective-permute-start | bytes 4423688 | tf_op jit(solution)/shard_map/ppermute | solution.py:16
  297.9 25.2 %collective-permute-done.17 = bf16[320,2304]{1,0:T(8,128)(2,1)S(1)} collective-permute-done((bf16[320,2304]{1,0:T(8,128)(2,1)S(1)}, bf16[320,2304]{1,0:T(8,128)(2,1)S(1)}, u32[]{:S(2)}, u32[]{:S(2)}) %collective-permute-start.17) | collective-permute-done | bytes 1474592 | tf_op jit(solution)/shard_map/ppermute | solution.py:20
  330.3 19.5 %all-to-all-done.1 = bf16[8,40,2304]{2,1,0:T(8,128)(2,1)S(1)} async-done(((bf16[8,40,2304]{2,1,0:T(8,128)(2,1)}), bf16[8,40,2304]{2,1,0:T(8,128)(2,1)S(1)}, u32[]{:S(2)}, u32[]{:S(2)}) %all-to-all-start.1) | async-done | bytes 1474592 | tf_op jit(solution)/shard_map/all_to_all | solution.py:168
  (105 shorter events, 66.7 us)
Async XLA Ops:
  0.0 329.8 %copy-start = (bf16[2304,8]{0,1:T(8,128)(2,1)S(1)}, bf16[2304,8]{0,1:T(8,128)(2,1)}, u32[]{:S(2)}) copy-start(bf16[2304,8]{0,1:T(8,128)(2,1)} %param.18) | copy-start | bytes 110596
  0.0 33.8 %copy-start.10 = (s32[1,128]{1,0:T(1,128)S(1)}, s32[1,128]{1,0:T(1,128)}, u32[]{:S(2)}) copy-start(s32[1,128]{1,0:T(1,128)} %param.15) | copy-start | bytes 1540
  0.0 22.0 %copy-start.4 = (bf16[1,128,2304]{2,1,0:T(8,128)(2,1)S(1)}, bf16[1,128,2304]{2,1,0:T(8,128)(2,1)}, u32[]{:S(2)}) copy-start(bf16[1,128,2304]{2,1,0:T(8,128)(2,1)} %param.12) | copy-start | bytes 1769476
  0.0 16.4 %collective-permute-start = (s32[128]{0:T(128)}, s32[128]{0:T(128)S(1)}, u32[]{:S(2)}, u32[]{:S(2)}) collective-permute-start(s32[128]{0:T(128)} %bitcast.96), channel_id=1, source_target_pairs={{0,8},{8,16},{16,24},{1,9},{9,17},{17,25},{2,10},{10,18},{18,26},{... | collective-permute-start | bytes 1544 | tf_op jit(solution)/shard_map/ppermute | solution.py:16
  5.1 29.0 %collective-permute-start.2 = (bf16[128,2304]{1,0:T(8,128)(2,1)}, bf16[128,2304]{1,0:T(8,128)(2,1)}, u32[]{:S(2)}, u32[]{:S(2)}) collective-permute-start(bf16[128,2304]{1,0:T(8,128)(2,1)} %bitcast.90), channel_id=1, source_target_pairs={{0,8},{8,16},{16,24},{1,9},{9,17},{17,25},{2,10},{10,18},{18,26},{... | collective-permute-start | bytes 1769480 | tf_op jit(solution)/shard_map/ppermute | solution.py:16
  9.4 33.7 %collective-permute-start.4 = (bf16[128,2304]{1,0:T(8,128)(2,1)}, bf16[128,2304]{1,0:T(8,128)(2,1)}, u32[]{:S(2)}, u32[]{:S(2)}) collective-permute-start(bf16[128,2304]{1,0:T(8,128)(2,1)} %bitcast.91), channel_id=1, source_target_pairs={{0,8},{8,16},{16,24},{1,9},{9,17},{17,25},{2,10},{10,18},{18,26},{... | collective-permute-start | bytes 1769480 | tf_op jit(solution)/shard_map/ppermute | solution.py:16
  16.4 17.4 %collective-permute-start.1 = (s32[128]{0:T(128)S(1)}, s32[128]{0:T(128)S(1)}, u32[]{:S(2)}, u32[]{:S(2)}) collective-permute-start(s32[128]{0:T(128)S(1)} %collective-permute-done), channel_id=1, source_target_pairs={{0,8},{8,16},{16,24},{1,9},{9,17},{17,25},{2,10},{10,18},{18,26},{... | collective-permute-start | bytes 1544 | tf_op jit(solution)/shard_map/ppermute | solution.py:16
  34.1 18.5 %collective-permute-start.3 = (bf16[128,2304]{1,0:T(8,128)(2,1)}, bf16[128,2304]{1,0:T(8,128)(2,1)}, u32[]{:S(2)}, u32[]{:S(2)}) collective-permute-start(bf16[128,2304]{1,0:T(8,128)(2,1)} %collective-permute-done.2), channel_id=1, source_target_pairs={{0,8},{8,16},{16,24},{1,9},{9,17},{17,25},{2,10},{10,18},{18,26},{... | collective-permute-start | bytes 1769480 | tf_op jit(solution)/shard_map/ppermute | solution.py:16
  45.2 17.6 %collective-permute-start.5 = (bf16[128,2304]{1,0:T(8,128)(2,1)}, bf16[128,2304]{1,0:T(8,128)(2,1)}, u32[]{:S(2)}, u32[]{:S(2)}) collective-permute-start(bf16[128,2304]{1,0:T(8,128)(2,1)} %collective-permute-done.4), channel_id=1, source_target_pairs={{0,8},{8,16},{16,24},{1,9},{9,17},{17,25},{2,10},{10,18},{18,26},{... | collective-permute-start | bytes 1769480 | tf_op jit(solution)/shard_map/ppermute | solution.py:16
  96.6 35.7 %collective-permute-start.6 = (bf16[320,2304]{1,0:T(8,128)(2,1)S(1)}, bf16[320,2304]{1,0:T(8,128)(2,1)}, u32[]{:S(2)}, u32[]{:S(2)}) collective-permute-start(bf16[320,2304]{1,0:T(8,128)(2,1)S(1)} %bitcast.86), channel_id=1, source_target_pairs={{0,8},{8,16},{16,24},{1,9},{9,17},{17,25},{2,10},{10,18},{18,26},{... | collective-permute-start | bytes 4423688 | tf_op jit(solution)/shard_map/ppermute | solution.py:16
  102.1 35.5 %collective-permute-start.7 = (bf16[320,2304]{1,0:T(8,128)(2,1)S(1)}, bf16[320,2304]{1,0:T(8,128)(2,1)}, u32[]{:S(2)}, u32[]{:S(2)}) collective-permute-start(bf16[320,2304]{1,0:T(8,128)(2,1)S(1)} %bitcast.87), channel_id=1, source_target_pairs={{8,0},{16,8},{24,16},{9,1},{17,9},{25,17},{10,2},{18,10},{26,18},{... | collective-permute-start | bytes 4423688 | tf_op jit(solution)/shard_map/ppermute | solution.py:20
  137.7 3.1 collective-permute-start.8
  139.4 35.1 %collective-permute-start.9 = (bf16[320,2304]{1,0:T(8,128)(2,1)}, bf16[320,2304]{1,0:T(8,128)(2,1)}, u32[]{:S(2)}, u32[]{:S(2)}) collective-permute-start(bf16[320,2304]{1,0:T(8,128)(2,1)} %collective-permute-done.7), channel_id=1, source_target_pairs={{8,0},{16,8},{9,1},{17,9},{10,2},{18,10},{11,3},{19,11},{12,4},{20... | collective-permute-start | bytes 4423688 | tf_op jit(solution)/shard_map/ppermute | solution.py:20
  174.6 20.7 %collective-permute-start.10 = (bf16[320,2304]{1,0:T(8,128)(2,1)}, bf16[320,2304]{1,0:T(8,128)(2,1)S(1)}, u32[]{:S(2)}, u32[]{:S(2)}) collective-permute-start(bf16[320,2304]{1,0:T(8,128)(2,1)} %collective-permute-done.8), channel_id=1, source_target_pairs={{16,24},{17,25},{18,26},{19,27},{20,28},{21,29},{22,30},{23,31}} | collective-permute-start | bytes 4423688 | tf_op jit(solution)/shard_map/ppermute | solution.py:16
  175.3 33.8 %collective-permute-start.11 = (bf16[320,2304]{1,0:T(8,128)(2,1)}, bf16[320,2304]{1,0:T(8,128)(2,1)S(1)}, u32[]{:S(2)}, u32[]{:S(2)}) collective-permute-start(bf16[320,2304]{1,0:T(8,128)(2,1)} %collective-permute-done.9), channel_id=1, source_target_pairs={{8,0},{9,1},{10,2},{11,3},{12,4},{13,5},{14,6},{15,7}} | collective-permute-start | bytes 4423688 | tf_op jit(solution)/shard_map/ppermute | solution.py:20
  226.1 29.9 %collective-permute-start.12 = (bf16[320,2304]{1,0:T(8,128)(2,1)S(1)}, bf16[320,2304]{1,0:T(8,128)(2,1)S(1)}, u32[]{:S(2)}, u32[]{:S(2)}) collective-permute-start(bf16[320,2304]{1,0:T(8,128)(2,1)S(1)} %fusion.17), channel_id=1, source_target_pairs={{0,8},{1,9},{2,10},{3,11},{4,12},{5,13},{6,14},{7,15}} | collective-permute-start | bytes 4423688 | tf_op jit(solution)/shard_map/ppermute | solution.py:16
  227.8 28.2 %collective-permute-start.15 = (bf16[320,2304]{1,0:T(8,128)(2,1)S(1)}, bf16[320,2304]{1,0:T(8,128)(2,1)S(1)}, u32[]{:S(2)}, u32[]{:S(2)}) collective-permute-start(bf16[320,2304]{1,0:T(8,128)(2,1)S(1)} %fusion.17), channel_id=1, source_target_pairs={{24,16},{25,17},{26,18},{27,19},{28,20},{29,21},{30,22},{31,23}} | collective-permute-start | bytes 4423688 | tf_op jit(solution)/shard_map/ppermute | solution.py:20
  256.7 31.8 %collective-permute-start.13 = (bf16[320,2304]{1,0:T(8,128)(2,1)S(1)}, bf16[320,2304]{1,0:T(8,128)(2,1)S(1)}, u32[]{:S(2)}, u32[]{:S(2)}) collective-permute-start(bf16[320,2304]{1,0:T(8,128)(2,1)S(1)} %get-tuple-element.26), channel_id=1, source_target_pairs={{0,8},{8,16},{1,9},{9,17},{2,10},{10,18},{3,11},{11,19},{4,12},{12... | collective-permute-start | bytes 4423688 | tf_op jit(solution)/shard_map/ppermute | solution.py:16
  261.2 15.7 %slice-start = ((s8[6635520]{0:T(1024)(128)(4,1)}), s8[4194304]{0:T(1024)(128)(4,1)S(1)}, s32[]{:S(2)}) async-start(s8[6635520]{0:T(1024)(128)(4,1)} %bitcast.102), calls=%async_computation.2 | async-start | bytes 8388608
  261.2 15.7 %slice-start.1 = ((s8[6635520]{0:T(1024)(128)(4,1)}), s8[2441216]{0:T(1024)(128)(4,1)S(1)}, s32[]{:S(2)}) async-start(s8[6635520]{0:T(1024)(128)(4,1)} %bitcast.102), calls=%async_computation.3 | async-start | bytes 4882432
  261.2 27.3 %collective-permute-start.16 = (bf16[320,2304]{1,0:T(8,128)(2,1)S(1)}, bf16[320,2304]{1,0:T(8,128)(2,1)S(1)}, u32[]{:S(2)}, u32[]{:S(2)}) collective-permute-start(bf16[320,2304]{1,0:T(8,128)(2,1)S(1)} %get-tuple-element.27), channel_id=1, source_target_pairs={{16,8},{24,16},{17,9},{25,17},{18,10},{26,18},{19,11},{27,19},{20,... | collective-permute-start | bytes 4423688 | tf_op jit(solution)/shard_map/ppermute | solution.py:20
  289.3 33.8 %collective-permute-start.17 = (bf16[320,2304]{1,0:T(8,128)(2,1)S(1)}, bf16[320,2304]{1,0:T(8,128)(2,1)S(1)}, u32[]{:S(2)}, u32[]{:S(2)}) collective-permute-start(bf16[320,2304]{1,0:T(8,128)(2,1)S(1)} %get-tuple-element.25), channel_id=1, source_target_pairs={{8,0},{16,8},{24,16},{9,1},{17,9},{25,17},{10,2},{18,10},{26,18},{... | collective-permute-start | bytes 4423688 | tf_op jit(solution)/shard_map/ppermute | solution.py:20
  290.6 33.7 %collective-permute-start.14 = (bf16[320,2304]{1,0:T(8,128)(2,1)S(1)}, bf16[320,2304]{1,0:T(8,128)(2,1)S(1)}, u32[]{:S(2)}, u32[]{:S(2)}) collective-permute-start(bf16[320,2304]{1,0:T(8,128)(2,1)S(1)} %get-tuple-element.24), channel_id=1, source_target_pairs={{0,8},{8,16},{16,24},{1,9},{9,17},{17,25},{2,10},{10,18},{18,26},{... | collective-permute-start | bytes 4423688 | tf_op jit(solution)/shard_map/ppermute | solution.py:16
  326.0 23.8 %all-to-all-start.1 = ((bf16[8,40,2304]{2,1,0:T(8,128)(2,1)}), bf16[8,40,2304]{2,1,0:T(8,128)(2,1)S(1)}, u32[]{:S(2)}, u32[]{:S(2)}) async-start(bf16[8,40,2304]{2,1,0:T(8,128)(2,1)} %bitcast.81), calls=%async_computation.1 | async-start | bytes 2949120 | tf_op jit(solution)/shard_map/all_to_all | solution.py:168
  (8 other events, 23.9 us)
